TPU v7x, 32 devices: a whole 2x2x4 slice. The times are simulated.
32 devices in a mesh: groups: 2 (over x), shot: 16 (over z, y, core).
Axes of the slice: x: 2, y: 2, z: 4, core: 2. Of those that a mesh axis runs over, the one named last changes fastest.
Arguments:
- speed_blocks: float32 [2048, 2048], P(('groups', 'shot')), parts along dimension 0, may hold values from 0.03 to 0.09
- aniso_blocks: float32 [2048, 2048], P(('groups', 'shot')), parts along dimension 0, may hold values from 0 to 0.25
- block_owner: int32 [4096, 1], P(('groups', 'shot')), parts along dimension 0, may hold values from 0 to 15; in each aligned block of 128 rows (0 to 127, 128 to 255, ...) at most 16 rows name the same one
- block_slot: int32 [4096], P(('groups', 'shot')), parts along dimension 0, may hold values from 0 to 63
- state_now: float32 [4096, 16, 128], P(('groups', 'shot')), parts along dimension 0, may hold values from -6 to 6
- state_prev: float32 [4096, 16, 128], P(('groups', 'shot')), parts along dimension 0, may hold values from -6 to 6
- adjoint_now: float32 [4096, 16, 128], P(('groups', 'shot')), parts along dimension 0, may hold values from -6 to 6
- adjoint_prev: float32 [4096, 16, 128], P(('groups', 'shot')), parts along dimension 0, may hold values from -6 to 6
- source_cell: int32 [32], P(('groups', 'shot')), parts along dimension 0, may hold values from 0 to 262143
- wavelet: float32 [32, 4], P(('groups', 'shot')), parts along dimension 0, may hold values from -8 to 8
- receiver_cell: int32 [32, 256], P(('groups', 'shot')), parts along dimension 0, may hold values from 0 to 262143
- observed: float32 [32, 4, 256], P(('groups', 'shot')), parts along dimension 0, may hold values from -6 to 6
Outputs:
- final_wave: float32 [4096, 16, 128], P(('groups', 'shot')), parts along dimension 0
- model_gradient: float32 [2048, 2, 2048], P(('groups', 'shot')), parts along dimension 0
There are 2 independent parts, one for each index of `groups`. A program takes and returns all parts, laid end to end along the dimension named above; each array names one. Nothing has to cross between parts.
Inputs may be any that keep to these rules, and one draw needn't show every extreme that they name: `block_owner`: among the 128 rows of one shot device no owner appears more than 16 times, and some owner appears exactly 16 times.
All inputs are finite; a program needn't handle non-finite values.
Results may differ from a plain program's by a relative error of at most 0.00017.
Values sent between devices are 32-bit elements; how exact they have to be, the bound alone decides.
No kernel may reach another device: no remote copies, remote signals or barrier semaphores. Data moves between devices by JAX's collectives and lax.ppermute only.
A program may use at most 128 MiB of HBM per device.

v0:
```python
import jax
import jax.numpy as jnp
from jax import lax
from jax.sharding import PartitionSpec as P

NEED = 128
STEPS = 4
SPLIT = 8
HALO = 5
MARGIN = 8

EDGE_SCALE = 0.02
KAPPA_RATE = 0.15
IMAGE_GAIN = 0.03125

HIGH = lax.Precision.HIGHEST


def neighbour_pairs(count):
    up = [(i, i + 1) for i in range(count - 1) if (i + SPLIT // 2) % SPLIT < SPLIT - 1]
    down = [(j, i) for i, j in up]
    return up, down


def exchange(top, bottom, count):
    up, down = neighbour_pairs(count)
    from_below = lax.ppermute(top, "shot", up)
    from_above = lax.ppermute(bottom, "shot", down)
    return from_below, from_above


def widen(own, below, above):
    gap = MARGIN - HALO
    rows, _, depth = own.shape
    zeros = jnp.zeros((rows, gap, depth), own.dtype)
    return jnp.concatenate([zeros, below, own, above, zeros], axis=1)


def shift_sum(v, axis):
    pad = [(0, 0)] * v.ndim
    pad[axis] = (1, 1)
    padded = jnp.pad(v, pad)
    length = v.shape[axis]
    return lax.slice_in_dim(padded, 2, length + 2, axis=axis) + lax.slice_in_dim(padded, 0, length, axis=axis)


def curvatures(v):
    horizontal = shift_sum(v, 0) + shift_sum(v, 1) - 4.0 * v
    vertical = shift_sum(v, 2) - 2.0 * v
    return horizontal, vertical


def cell_coords(cell, cross, offset):
    x = cell // (cross * 128)
    y = (cell // 128) % cross + offset
    z = cell % 128
    return x, y, z


def add_at(field, xs, ys, zs, values):
    wide = field.shape[1]
    valid = (ys >= 0) & (ys < wide)
    ys = jnp.where(valid, ys, wide + 1024)
    return field.at[xs, ys, zs].add(values, mode="drop")


def shards(
    speed_blocks,
    aniso_blocks,
    block_owner,
    block_slot,
    state_now,
    state_prev,
    adjoint_now,
    adjoint_prev,
    source_cell,
    wavelet,
    receiver_cell,
    observed,
):
    count = lax.axis_size("shot")
    me = lax.axis_index("shot")
    capacity = 2 * NEED // count
    slots_all = count * capacity
    rows, cross, depth = state_now.shape
    row_len = cross * depth
    owned = speed_blocks.shape[0]
    nrec = receiver_cell.shape[1]

    info = jnp.concatenate(
        [
            source_cell.astype(jnp.float32),
            wavelet[0],
            receiver_cell[0].astype(jnp.float32),
        ]
    )
    info = jnp.pad(info, (0, rows * depth - info.shape[0])).reshape(rows, 1, depth)
    fields = (state_now, state_prev, adjoint_now, adjoint_prev)
    top = jnp.concatenate([f[:, cross - HALO :] for f in fields] + [info], axis=1)
    bottom = jnp.concatenate([f[:, :HALO] for f in fields] + [info], axis=1)
    from_below, from_above = exchange(top, bottom, count)

    owners = block_owner[:, 0]
    column_ids = jnp.arange(count, dtype=jnp.int32)
    onehot = (owners[:, None] == column_ids[None, :]).astype(jnp.int32)
    before_count = jnp.sum((jnp.cumsum(onehot, axis=0) - onehot) * onehot, axis=1)
    placed = owners * capacity + before_count
    requests = jnp.full((slots_all,), -1, jnp.int32).at[placed].set(block_slot)
    wanted = lax.all_to_all(
        requests.reshape(count, capacity), "shot", split_axis=0, concat_axis=0, tiled=True
    ).reshape(-1)

    owned_rows = jnp.concatenate([speed_blocks, aniso_blocks], axis=1)
    pick = (wanted[:, None] == jnp.arange(owned, dtype=jnp.int32)[None, :]).astype(jnp.float32)
    outgoing = jnp.dot(pick, owned_rows, precision=HIGH)
    incoming = lax.all_to_all(
        outgoing.reshape(count, capacity, 2 * row_len),
        "shot",
        split_axis=0,
        concat_axis=0,
        tiled=True,
    ).reshape(slots_all, 2 * row_len)
    place_hot = (placed[:, None] == jnp.arange(slots_all, dtype=jnp.int32)[None, :]).astype(
        jnp.float32
    )
    fetched = jnp.dot(place_hot, incoming, precision=HIGH)
    speed_own = fetched[:, :row_len].reshape(rows, cross, depth)
    aniso_own = fetched[:, row_len:].reshape(rows, cross, depth)

    model_below, model_above = exchange(
        jnp.concatenate([speed_own[:, cross - HALO :], aniso_own[:, cross - HALO :]], axis=1),
        jnp.concatenate([speed_own[:, :HALO], aniso_own[:, :HALO]], axis=1),
        count,
    )
    speeds = widen(speed_own, model_below[:, :HALO], model_above[:, :HALO])
    hfactor = 1.0 + 2.0 * widen(aniso_own, model_below[:, HALO:], model_above[:, HALO:])

    def part(received, k):
        return received[:, k * HALO : (k + 1) * HALO]

    wide_fields = [widen(f, part(from_below, k), part(from_above, k)) for k, f in enumerate(fields)]
    info_below = from_below[:, 4 * HALO].reshape(-1)
    info_above = from_above[:, 4 * HALO].reshape(-1)

    def unpack(flat):
        src = flat[0].astype(jnp.int32)
        wav = flat[1 : 1 + STEPS]
        rec = flat[1 + STEPS : 1 + STEPS + nrec].astype(jnp.int32)
        return src, wav, rec

    src_below, wav_below, rec_below = unpack(info_below)
    src_above, wav_above, rec_above = unpack(info_above)

    lower_offset = MARGIN - cross
    upper_offset = MARGIN + cross
    sx, sy, sz = [
        jnp.stack(parts)
        for parts in zip(
            cell_coords(source_cell[0], cross, MARGIN),
            cell_coords(src_below, cross, lower_offset),
            cell_coords(src_above, cross, upper_offset),
        )
    ]
    wav_all = jnp.stack([wavelet[0], wav_below, wav_above], axis=1)
    rx_own, ry_own, rz_own = cell_coords(receiver_cell[0], cross, MARGIN)
    rx, ry, rz = [
        jnp.concatenate(parts)
        for parts in zip(
            (rx_own, ry_own, rz_own),
            cell_coords(rec_below, cross, lower_offset),
            cell_coords(rec_above, cross, upper_offset),
        )
    ]

    previous, current, later_adjoint, adjoint = wide_fields[1], wide_fields[0], wide_fields[3], wide_fields[2]
    waves = []
    misfits = []
    for time_step in range(STEPS):
        horizontal, vertical = curvatures(current)
        advanced = 2.0 * current - previous + speeds * (hfactor * horizontal + vertical)
        advanced = add_at(advanced, sx, sy, sz, wav_all[time_step])
        synthetic = advanced[rx_own, ry_own, rz_own]
        misfits.append(synthetic - observed[0, time_step])
        waves.append(current)
        previous, current = current, advanced
    final_wave = current[:, MARGIN : MARGIN + cross]

    misfit_own = jnp.stack(misfits)
    mis_below, mis_above = exchange(misfit_own, misfit_own, count)

    image_horizontal = jnp.zeros_like(current)
    image_vertical = jnp.zeros_like(current)
    for time_step in range(STEPS - 1, -1, -1):
        horizontal, vertical = curvatures(adjoint)
        earlier = 2.0 * adjoint - later_adjoint + speeds * (hfactor * horizontal + vertical)
        injected = jnp.concatenate(
            [misfit_own[time_step], mis_below[time_step], mis_above[time_step]]
        )
        earlier = add_at(earlier, rx, ry, rz, injected)
        wave_horizontal, wave_vertical = curvatures(waves[time_step])
        image_horizontal = image_horizontal + earlier * wave_horizontal
        image_vertical = image_vertical + earlier * wave_vertical
        later_adjoint, adjoint = adjoint, earlier

    gradient_speed = hfactor * image_horizontal + image_vertical
    gradient_aniso = 2.0 * speeds * image_horizontal

    position = (me + SPLIT // 2) % SPLIT
    has_below = jnp.logical_and(position > 0, me > 0).astype(jnp.float32)
    has_above = jnp.logical_and(position < SPLIT - 1, me < count - 1).astype(jnp.float32)
    wide = speeds.shape[1]
    layer = lax.broadcasted_iota(jnp.int32, (1, wide, 1), 1)
    exists = jnp.where(
        layer < MARGIN, has_below, jnp.where(layer >= MARGIN + cross, has_above, 1.0)
    )
    exists = jnp.broadcast_to(exists, speeds.shape)

    lo, hi = MARGIN, MARGIN + cross
    grads = jnp.stack([gradient_speed, gradient_aniso])
    center_g = grads[:, :, lo:hi]
    center_s = speeds[:, lo:hi]

    def neighbour(v, axis, step):
        nd = v.ndim
        ax = nd - 3 + axis
        if axis == 1:
            return lax.slice_in_dim(v, lo + step, hi + step, axis=ax)
        center = lax.slice_in_dim(v, lo, hi, axis=nd - 2)
        pad = [(0, 0)] * nd
        pad[ax] = (1, 1)
        padded = jnp.pad(center, pad)
        length = center.shape[ax]
        return lax.slice_in_dim(padded, 1 + step, 1 + step + length, axis=ax)

    totals = jnp.zeros_like(center_g)
    for axis in (0, 1, 2):
        for step in (1, -1):
            g_n = neighbour(grads, axis, step)
            s_n = neighbour(speeds, axis, step)
            e_n = neighbour(exists, axis, step)
            contrast = (s_n - center_s) / EDGE_SCALE
            weight = e_n / (1.0 + contrast * contrast)
            totals = totals + weight[None] * (g_n - center_g)
    smoothed = center_g + KAPPA_RATE * totals

    rows_out = jnp.transpose(smoothed, (1, 0, 2, 3)).reshape(rows, 2 * row_len)
    returning = jnp.dot(place_hot.T, rows_out, precision=HIGH)
    returned = lax.all_to_all(
        returning.reshape(count, capacity, 2 * row_len),
        "shot",
        split_axis=0,
        concat_axis=0,
        tiled=True,
    ).reshape(slots_all, 2 * row_len)
    summed = jnp.dot(pick.T, returned, precision=HIGH)
    return (final_wave, (summed * IMAGE_GAIN).reshape(owned, 2, row_len))


def solution(mesh):
    placed = (
        P(("groups", "shot"), None),
        P(("groups", "shot"), None),
        P(("groups", "shot"), None),
        P(("groups", "shot")),
        P(("groups", "shot"), None, None),
        P(("groups", "shot"), None, None),
        P(("groups", "shot"), None, None),
        P(("groups", "shot"), None, None),
        P(("groups", "shot")),
        P(("groups", "shot"), None),
        P(("groups", "shot"), None),
        P(("groups", "shot"), None, None),
    )
    return jax.shard_map(
        shards,
        mesh=mesh,
        in_specs=placed,
        out_specs=(P(("groups", "shot"), None, None), P(("groups", "shot"), None, None)),
        check_vma=False,
    )
```

profile of v0, /device:TPU:13, one launch (start us, length us, event | category | flops | bytes accessed | tf_op | source)
XLA Modules:
  0.0 898.4 jit_solution(4951942093213319517)
XLA Ops:
  2.4 1.3 fusion.137
  3.6 1.1 scatter_custom_fusion
  4.8 10.2 %all_to_all.19 = s32[16,1,16]{2,1,0:T(1,128)S(1)} all-to-all(s32[16,1,16]{2,1,0:T(1,128)S(1)} %all_to_all.12), channel_id=1, replica_groups=mesh['groups'=2,'shot'=16] {'shot'}, dimensions={0} | all-to-all | bytes 2048 | tf_op jit(solution)/shard_map/all_to_all | solution.py:109
  16.3 5.1 fusion.95
  21.3 7.2 all-to-all-start.1
  29.4 1.0 copy_dynamic-update-slice_fusion.3
  36.1 2.3 collective-permute-start.1
  38.4 4.2 collective-permute-start
  45.1 90.7 %collective-permute-done.1 = f32[128,21,128]{2,0,1:T(8,128)} collective-permute-done((f32[128,21,128]{2,0,1:T(8,128)}, f32[128,21,128]{2,0,1:T(8,128)}, u32[]{:S(2)}, u32[]{:S(2)}) %collective-permute-start.1) | collective-permute-done | bytes 1376288 | tf_op jit(solution)/shard_map/ppermute | solution.py:28
  140.0 2.2 fusion.143
  142.2 1.0 copy.46
  143.2 2.2 fusion.142
  145.5 1.0 copy.51
  146.5 1.0 copy.52
  147.5 1.0 copy.53
  148.5 2.0 copy.58
  150.5 2.0 copy.59
  152.5 2.0 copy.60
  154.5 2.0 copy.61
  156.5 5.4 concatenate.216
  161.9 5.4 concatenate.217
  167.3 5.5 concatenate.224
  172.8 3.6 concatenate.225
  177.2 3.9 fusion.99
  183.0 1.9 collective-permute-start.2
  185.4 2.6 collective-permute-start.3
  188.3 4.1 collective-permute-done.2
  192.7 5.5 collective-permute-done.3
  198.5 1.1 copy.56
  199.6 1.0 copy.57
  200.6 3.6 concatenate.221
  204.2 4.4 concatenate.222
  208.6 11.4 %multiply_add_fusion.4 = (f32[128,32,128]{2,1,0:T(8,128)}, f32[128,32,128]{2,1,0:T(8,128)}) fusion(f32[128,32,128]{2,1,0:T(8,128)} %concatenate.221, f32[128,32,128]{2,1,0:T(8,128)} %concatenate.217, f32[128,32,128]{2,1,0:T(8,128)} %concatenate.216, f32[128,32,128]{2,1,0:T(8,128)S(1)} %concatenate.222), kind=kLoop, calls=%fused_computation.136 | loop fusion | flops 7864320 | bytes 12582912 | tf_op jit(solution)/shard_map/add | solution.py:180
  220.0 2.0 scatter_fusion
  222.0 11.0 %multiply_add_fusion.3 = (f32[128,32,128]{2,1,0:T(8,128)}, f32[128,32,128]{2,1,0:T(8,128)}) fusion(f32[128,32,128]{2,1,0:T(8,128)} %concatenate.221, f32[128,32,128]{2,1,0:T(8,128)} %concatenate.216, f32[128,32,128]{2,1,0:T(8,128)} %scatter_fusion, f32[128,32,128]{2,1,0:T(8,128)S(1)} %concatenate.222), kind=kLoop, calls=%fused_computation.135 | loop fusion | flops 7864320 | bytes 12582912 | tf_op jit(solution)/shard_map/add | solution.py:180
  233.0 2.0 scatter_fusion.1
  234.9 11.3 %multiply_add_fusion.2 = (f32[128,32,128]{2,1,0:T(8,128)}, f32[128,32,128]{2,1,0:T(8,128)}) fusion(f32[128,32,128]{2,1,0:T(8,128)} %concatenate.221, f32[128,32,128]{2,1,0:T(8,128)} %scatter_fusion, f32[128,32,128]{2,1,0:T(8,128)} %scatter_fusion.1, f32[128,32,128]{2,1,0:T(8,128)S(1)} %concatenate.222), kind=kLoop, calls=%fused_computation.134 | loop fusion | flops 7864320 | bytes 12582912 | tf_op jit(solution)/shard_map/add | solution.py:180
  246.3 3.6 gather_fusion.1
  249.9 3.6 gather_fusion.2
  253.6 2.0 scatter_fusion.2
  255.5 3.7 gather_fusion.3
  259.2 18.9 %multiply_add_fusion.1 = (f32[128,32,128]{2,1,0:T(8,128)}, f32[128,32,128]{2,1,0:T(8,128)}, f32[128,32,128]{2,1,0:T(8,128)}) fusion(f32[128,32,128]{2,1,0:T(8,128)} %concatenate.221, f32[128,32,128]{2,1,0:T(8,128)} %scatter_fusion.1, f32[128,32,128]{2,1,0:T(8,128)} %scatter_fusion.2, f32[128,32,128]{2,1,0:T(8,128)S(1)} %concatenate.222, ...), kind=kLoop, calls=%fused_computation.133 | loop fusion | flops 14680064 | bytes 18874368 | tf_op jit(solution)/shard_map/add | solution.py:180
  278.2 2.0 scatter_fusion.3
  280.1 3.6 gather_fusion
  283.8 1.9 collective-permute-start.5
  285.7 4.8 collective-permute-start.4
  290.7 4.6 fusion.73
  295.4 105.7 %scatter_fusion.4 = f32[128,32,128]{2,1,0:T(8,128)} fusion(f32[128,32,128]{2,1,0:T(8,128)} %get-tuple-element.16, s32[768]{0:T(1024)S(1)} %fusion.113, f32[768]{0:T(1024)S(1)} %pad_maximum_fusion.6), kind=kCustom, calls=%fused_computation.9 | custom fusion | flops 768 | bytes 18432 | tf_op jit(solution)/shard_map/scatter-add | solution.py:64
  401.1 11.0 %fusion.25 = f32[128,32,128]{2,1,0:T(8,128)} fusion(f32[128,32,128]{2,1,0:T(8,128)} %concatenate.221, f32[128,32,128]{2,1,0:T(8,128)} %scatter_fusion.4, f32[128,32,128]{2,1,0:T(8,128)} %concatenate.224, f32[128,32,128]{2,1,0:T(8,128)S(1)} %concatenate.222), kind=kLoop, calls=%fused_computation.81 | loop fusion | flops 7864320 | bytes 10485760 | tf_op jit(solution)/shard_map/add | solution.py:195
  412.1 105.4 %scatter_fusion.5 = f32[128,32,128]{2,1,0:T(8,128)} fusion(f32[128,32,128]{2,1,0:T(8,128)} %fusion.25, s32[768]{0:T(1024)S(1)} %fusion.113, f32[768]{0:T(1024)S(1)} %pad_maximum_fusion.7), kind=kCustom, calls=%fused_computation.10 | custom fusion | flops 768 | bytes 18432 | tf_op jit(solution)/shard_map/scatter-add | solution.py:64
  517.5 11.2 %fusion.32 = f32[128,32,128]{2,1,0:T(8,128)} fusion(f32[128,32,128]{2,1,0:T(8,128)} %concatenate.221, f32[128,32,128]{2,1,0:T(8,128)} %scatter_fusion.5, f32[128,32,128]{2,1,0:T(8,128)} %scatter_fusion.4, f32[128,32,128]{2,1,0:T(8,128)S(1)} %concatenate.222), kind=kLoop, calls=%fused_computation.88 | loop fusion | flops 7864320 | bytes 10485760 | tf_op jit(solution)/shard_map/add | solution.py:195
  528.8 105.8 %scatter_fusion.6 = f32[128,32,128]{2,1,0:T(8,128)} fusion(f32[128,32,128]{2,1,0:T(8,128)} %fusion.32, s32[768]{0:T(1024)S(1)} %fusion.113, f32[768]{0:T(1024)S(1)} %pad_maximum_fusion.8), kind=kCustom, calls=%fused_computation.11 | custom fusion | flops 768 | bytes 18432 | tf_op jit(solution)/shard_map/scatter-add | solution.py:64
  634.6 10.8 %fusion.39 = f32[128,32,128]{2,1,0:T(8,128)} fusion(f32[128,32,128]{2,1,0:T(8,128)} %concatenate.221, f32[128,32,128]{2,1,0:T(8,128)} %scatter_fusion.6, f32[128,32,128]{2,1,0:T(8,128)} %scatter_fusion.5, f32[128,32,128]{2,1,0:T(8,128)S(1)} %concatenate.222), kind=kLoop, calls=%fused_computation.95 | loop fusion | flops 7864320 | bytes 10485760 | tf_op jit(solution)/shard_map/add | solution.py:195
  645.3 105.8 %scatter_fusion.7 = f32[128,32,128]{2,1,0:T(8,128)} fusion(f32[128,32,128]{2,1,0:T(8,128)} %fusion.39, s32[768]{0:T(1024)S(1)} %fusion.113, f32[768]{0:T(1024)S(1)} %pad_maximum_fusion.9), kind=kCustom, calls=%fused_computation.12 | custom fusion | flops 768 | bytes 18432 | tf_op jit(solution)/shard_map/scatter-add | solution.py:64
  751.1 11.1 %multiply_bitcast_fusion = (f32[1,128,32,128]{3,2,1,0:T(8,128)}, f32[128,32,128]{2,1,0:T(8,128)}) fusion(f32[128,32,128]{2,1,0:T(8,128)} %concatenate.221, f32[128,32,128]{2,1,0:T(8,128)} %scatter_fusion.7, f32[128,32,128]{2,1,0:T(8,128)} %get-tuple-element.15, f32[128,32,128]{2,1,0:T(8,128)} %scatter_fusion.6, f32[128,32,128]{2,1,0:T(8,128)} %get-tuple-element.13, ...), kind=kLoop, calls=%fused_computation.130 | loop fusion | flops 4718592 | bytes 23068672 | tf_op jit(solution)/shard_map/stack | solution.py:219
  762.2 15.1 %add_bitcast_fusion = f32[1,128,32,128]{3,2,1,0:T(8,128)S(1)} fusion(f32[128,32,128]{2,1,0:T(8,128)} %scatter_fusion.7, f32[128,32,128]{2,1,0:T(8,128)S(1)} %copy-done.2, f32[128,32,128]{2,1,0:T(8,128)S(1)} %copy-done.1, f32[128,32,128]{2,1,0:T(8,128)S(1)} %copy-done, f32[128,32,128]{2,1,0:T(8,128)} %get-tuple-element.7, ...), kind=kLoop, calls=%fused_computation.131 | loop fusion | flops 12058624 | bytes 23068672 | tf_op jit(solution)/shard_map/stack | solution.py:219
  780.2 2.4 fusion.62
  782.7 1.9 copy.38
  784.6 5.5 fusion.100
  790.0 9.7 %all-to-all-start.2 = ((f32[16,16,4096]{2,1,0:T(8,128)}), f32[16,16,4096]{2,1,0:T(8,128)}, u32[]{:S(2)}, u32[]{:S(2)}) async-start(f32[16,16,4096]{2,1,0:T(8,128)} %fusion.100), calls=%async_computation.2 | async-start | bytes 8388608 | tf_op jit(solution)/shard_map/all_to_all | solution.py:248
  799.7 1.1 slice.580
  800.8 91.4 %all-to-all-done.2 = f32[16,16,4096]{2,1,0:T(8,128)} async-done(((f32[16,16,4096]{2,1,0:T(8,128)}), f32[16,16,4096]{2,1,0:T(8,128)}, u32[]{:S(2)}, u32[]{:S(2)}) %all-to-all-start.2) | async-done | bytes 4194336 | tf_op jit(solution)/shard_map/all_to_all | solution.py:248
  892.2 3.9 convolution_multiply_fusion
  896.1 1.9 reshape.1096
  (148 shorter events, 21.1 us)
Async XLA Ops:
  16.3 5.1 copy-start.24
  21.3 7.2 copy-start.23
  21.3 7.9 copy-start.14
  21.3 155.9 %all-to-all-start.1 = ((f32[16,16,4096]{2,1,0:T(8,128)}), f32[16,16,4096]{2,1,0:T(8,128)}, u32[]{:S(2)}, u32[]{:S(2)}) async-start(f32[16,16,4096]{2,1,0:T(8,128)} %bitcast.127), calls=%async_computation.1 | async-start | bytes 8388608 | tf_op jit(solution)/shard_map/all_to_all | solution.py:116
  28.5 1.8 copy-start.15
  29.4 1.9 copy-start.16
  30.4 1.7 copy-start.17
  32.2 3.2 copy-start.34
  32.2 12.3 %copy-start.22 = (f32[1,4,256]{2,1,0:T(4,128)S(1)}, f32[1,4,256]{2,1,0:T(4,128)}, u32[]{:S(2)}) copy-start(f32[1,4,256]{2,1,0:T(4,128)} %param.23) | copy-start | bytes 12292
  36.1 99.7 %collective-permute-start.1 = (f32[128,21,128]{2,0,1:T(8,128)}, f32[128,21,128]{2,0,1:T(8,128)}, u32[]{:S(2)}, u32[]{:S(2)}) collective-permute-start(f32[128,21,128]{2,0,1:T(8,128)} %get-tuple-element.71), channel_id=1, source_target_pairs={{1,0},{2,1},{3,2},{5,4},{6,5},{7,6},{8,7},{9,8},{10,9},{11,10},{13... | collective-permute-start | bytes 4128776 | tf_op jit(solution)/shard_map/ppermute | solution.py:28
  38.4 99.5 %collective-permute-start = (f32[128,21,128]{2,0,1:T(8,128)}, f32[128,21,128]{2,0,1:T(8,128)}, u32[]{:S(2)}, u32[]{:S(2)}) collective-permute-start(f32[128,21,128]{2,0,1:T(8,128)} %get-tuple-element.72), channel_id=1, source_target_pairs={{0,1},{1,2},{2,3},{4,5},{5,6},{6,7},{7,8},{8,9},{9,10},{10,11},{12... | collective-permute-start | bytes 4128776 | tf_op jit(solution)/shard_map/ppermute | solution.py:27
  167.3 5.5 copy-start.18
  167.3 5.5 copy-start.19
  167.3 5.5 copy-start.20
  172.8 3.8 copy-start.32
  172.8 3.8 copy-start.33
  172.8 4.4 copy-start.26
  181.7 1.0 copy-start.5
  183.0 5.1 copy-start.35
  183.0 5.1 copy-start.39
  183.0 9.4 %collective-permute-start.2 = (f32[128,10,128]{2,0,1:T(8,128)S(1)}, f32[128,10,128]{2,0,1:T(8,128)S(1)}, u32[]{:S(2)}, u32[]{:S(2)}) collective-permute-start(f32[128,10,128]{2,0,1:T(8,128)S(1)} %copy.28), channel_id=1, source_target_pairs={{0,1},{1,2},{2,3},{4,5},{5,6},{6,7},{7,8},{8,9},{9,10},{10,11},{12... | collective-permute-start | bytes 1966088 | tf_op jit(solution)/shard_map/ppermute | solution.py:27
  185.4 12.8 %collective-permute-start.3 = (f32[128,10,128]{2,0,1:T(8,128)S(1)}, f32[128,10,128]{2,0,1:T(8,128)S(1)}, u32[]{:S(2)}, u32[]{:S(2)}) collective-permute-start(f32[128,10,128]{2,0,1:T(8,128)S(1)} %copy.30), channel_id=1, source_target_pairs={{1,0},{2,1},{3,2},{5,4},{6,5},{7,6},{8,7},{9,8},{10,9},{11,10},{13... | collective-permute-start | bytes 1966088 | tf_op jit(solution)/shard_map/ppermute | solution.py:28
  192.7 7.9 copy-start.6
  198.5 2.1 copy-start.7
  278.1 12.4 %copy-start.38 = (f32[16]{0:T(128)S(1)}, f32[16]{0:T(128)}, u32[]{:S(2)}) copy-start(f32[16]{0:T(128)} %get-tuple-element.80) | copy-start | bytes 196
  278.1 12.5 %copy-start.36 = (f32[16]{0:T(128)S(1)}, f32[16]{0:T(128)}, u32[]{:S(2)}) copy-start(f32[16]{0:T(128)} %get-tuple-element.78) | copy-start | bytes 196
  278.1 12.5 %copy-start.37 = (f32[16]{0:T(128)S(1)}, f32[16]{0:T(128)}, u32[]{:S(2)}) copy-start(f32[16]{0:T(128)} %get-tuple-element.79) | copy-start | bytes 196
  283.8 11.5 %collective-permute-start.5 = (f32[4,256]{1,0:T(4,128)S(1)}, f32[4,256]{1,0:T(4,128)S(1)}, u32[]{:S(2)}, u32[]{:S(2)}) collective-permute-start(f32[4,256]{1,0:T(4,128)S(1)} %pad_maximum_fusion.5), channel_id=1, source_target_pairs={{1,0},{2,1},{3,2},{5,4},{6,5},{7,6},{8,7},{9,8},{10,9},{11,10},{13... | collective-permute-start | bytes 12296 | tf_op jit(solution)/shard_map/ppermute | solution.py:28
  285.7 9.6 %collective-permute-start.4 = (f32[4,256]{1,0:T(4,128)S(1)}, f32[4,256]{1,0:T(4,128)S(1)}, u32[]{:S(2)}, u32[]{:S(2)}) collective-permute-start(f32[4,256]{1,0:T(4,128)S(1)} %pad_maximum_fusion.5), channel_id=1, source_target_pairs={{0,1},{1,2},{2,3},{4,5},{5,6},{6,7},{7,8},{8,9},{9,10},{10,11},{12... | collective-permute-start | bytes 12296 | tf_op jit(solution)/shard_map/ppermute | solution.py:27
  290.7 4.6 copy-start.31
  290.7 4.6 copy-start.30
  290.7 4.6 copy-start.29
  290.7 4.6 copy-start.28
  751.1 11.1 %copy-start = (f32[128,32,128]{2,1,0:T(8,128)S(1)}, f32[128,32,128]{2,1,0:T(8,128)}, u32[]{:S(2)}) copy-start(f32[128,32,128]{2,1,0:T(8,128)} %scatter_fusion.4) | copy-start | bytes 6291460
  751.1 11.1 %copy-start.1 = (f32[128,32,128]{2,1,0:T(8,128)S(1)}, f32[128,32,128]{2,1,0:T(8,128)}, u32[]{:S(2)}) copy-start(f32[128,32,128]{2,1,0:T(8,128)} %scatter_fusion.5) | copy-start | bytes 6291460
  751.1 11.1 %copy-start.2 = (f32[128,32,128]{2,1,0:T(8,128)S(1)}, f32[128,32,128]{2,1,0:T(8,128)}, u32[]{:S(2)}) copy-start(f32[128,32,128]{2,1,0:T(8,128)} %scatter_fusion.6) | copy-start | bytes 6291460
  762.2 15.2 %copy-start.3 = (f32[1,128,32,128]{3,2,1,0:T(8,128)S(1)}, f32[1,128,32,128]{3,2,1,0:T(8,128)}, u32[]{:S(2)}) copy-start(f32[1,128,32,128]{3,2,1,0:T(8,128)} %get-tuple-element.6) | copy-start | bytes 6291460
  777.4 1.2 copy-start.8
  777.4 1.5 copy-start.9
  777.4 1.8 copy-start.10
  777.4 2.1 copy-start.11
  777.4 2.5 copy-start.12
  777.5 2.8 copy-start.13
  782.7 1.9 copy-start.21
  782.7 1.9 copy-start.27
  790.0 9.7 %copy-start.4 = (f32[128,32,128]{2,1,0:T(8,128)S(1)}, f32[128,32,128]{2,1,0:T(8,128)}, u32[]{:S(2)}) copy-start(f32[128,32,128]{2,1,0:T(8,128)} %scatter_fusion.3) | copy-start | bytes 6291460
  790.0 102.1 %all-to-all-start.2 = ((f32[16,16,4096]{2,1,0:T(8,128)}), f32[16,16,4096]{2,1,0:T(8,128)}, u32[]{:S(2)}, u32[]{:S(2)}) async-start(f32[16,16,4096]{2,1,0:T(8,128)} %fusion.100), calls=%async_computation.2 | async-start | bytes 8388608 | tf_op jit(solution)/shard_map/all_to_all | solution.py:248
  799.7 92.5 %copy-start.25 = (s32[256]{0:T(256)S(1)}, s32[256]{0:T(256)}, u32[]{:S(2)}) copy-start(s32[256]{0:T(256)} %copy-done.24) | copy-start | bytes 3076
where the time goes:
time: 915 us; the launch traced here: 898 us
  other arithmetic  556 us (61%)
  waiting for transfers between devices  192 us (21%)
  local copies, waits for them, and re-layouts  83.6 us (9%)
  starting transfers between devices  34.5 us (4%)
  matrix products  18.4 us (2%)
  blocking collectives  10.2 us (1%)
    scatter-add x8, other arithmetic, add_at(): return field.at[xs, ys, zs].add(values, mode='drop')  431 us
    ppermute x3, waiting for transfers between devices, exchange(): from_above = lax.ppermute(bottom, 'shot', down)  96.2 us
    all_to_all x1, waiting for transfers between devices, shards(): lax.all_to_all(returning.reshape(count, capacity, 2 * row_len), 'shot', s...  91.4 us
    add x4, other arithmetic, shards(): 2.0 * current - previous + speeds * (hfactor * horizontal + vertical)  52.7 us
    add x3, other arithmetic, shards(): 2.0 * adjoint - later_adjoint + speeds * (hfactor * horizontal + vertical)  33 us
    concatenate x6, local copies, waits for them, and re-layouts, widen(): return jnp.concatenate([zeros, below, own, above, zeros], axis=1)  27.9 us
    another operation x3, other arithmetic, shards(): grads = jnp.stack([gradient_speed, gradient_aniso])  26.5 us
    unnamed x102, local copies, waits for them, and re-layouts  24.2 us
  transfers between devices with their start and end apart: 8, of which 4 were waited for; matrix products, arithmetic and copies ran while one was open for 6% of the time, Pallas kernels for 0%

commit v1 on v0

--- a/solution.py
+++ b/solution.py
@@ -2,6 +2,8 @@
 import jax.numpy as jnp
 from jax import lax
 from jax.sharding import PartitionSpec as P
+from jax.experimental import pallas as pl
+from jax.experimental.pallas import tpu as pltpu
 
 NEED = 128
 STEPS = 4
@@ -62,6 +64,216 @@
     valid = (ys >= 0) & (ys < wide)
     ys = jnp.where(valid, ys, wide + 1024)
     return field.at[xs, ys, zs].add(values, mode="drop")
+
+
+CX = 4
+
+
+def stencil(c, xp, xm):
+    n_y, n_z = c.shape[1], c.shape[2]
+    lane = lax.broadcasted_iota(jnp.int32, c.shape, 2)
+    yp = pltpu.roll(c, n_y - 1, 1)
+    ym = pltpu.roll(c, 1, 1)
+    zp = jnp.where(lane == n_z - 1, 0.0, pltpu.roll(c, n_z - 1, 2))
+    zm = jnp.where(lane == 0, 0.0, pltpu.roll(c, 1, 2))
+    horizontal = (xp + xm) + (yp + ym) - 4.0 * c
+    vertical = (zp + zm) - 2.0 * c
+    return horizontal, vertical
+
+
+def step_pass(buf, cur, prev, new, sp, hf):
+    rows = sp.shape[0]
+
+    def body(i, carry):
+        x0 = pl.multiple_of(i * CX, CX)
+        c = buf[cur, pl.ds(x0 + 1, CX)]
+        horizontal, vertical = stencil(c, buf[cur, pl.ds(x0 + 2, CX)], buf[cur, pl.ds(x0, CX)])
+        advanced = 2.0 * c - buf[prev, pl.ds(x0 + 1, CX)] + sp[pl.ds(x0, CX)] * (
+            hf[pl.ds(x0, CX)] * horizontal + vertical
+        )
+        buf[new, pl.ds(x0 + 1, CX)] = advanced
+        return carry
+
+    lax.fori_loop(0, rows // CX, body, 0)
+
+
+def add_points(buf, slot, coords, vals, base, count):
+    depth = buf.shape[-1]
+    sub = lax.broadcasted_iota(jnp.int32, (8, depth), 0)
+    lane = lax.broadcasted_iota(jnp.int32, (8, depth), 1)
+
+    def body(k, carry):
+        x = coords[3 * k]
+        y = coords[3 * k + 1]
+        z = coords[3 * k + 2]
+        val = vals[base + k]
+        y8 = pl.multiple_of((y // 8) * 8, 8)
+        tile = buf[slot, x + 1, pl.ds(y8, 8), :]
+        hit = (sub == y - y8) & (lane == z)
+        buf[slot, x + 1, pl.ds(y8, 8), :] = tile + jnp.where(hit, val, 0.0)
+        return carry
+
+    lax.fori_loop(0, count, body, 0)
+
+
+def load_padded(buf, slot, field):
+    rows = field.shape[0]
+
+    def body(i, carry):
+        x0 = pl.multiple_of(i * CX, CX)
+        buf[slot, pl.ds(x0 + 1, CX)] = field[pl.ds(x0, CX)]
+        return carry
+
+    lax.fori_loop(0, rows // CX, body, 0)
+
+
+def zero_edges(buf):
+    zero = jnp.zeros(buf.shape[2:], jnp.float32)
+    for slot in range(buf.shape[0]):
+        buf[slot, 0] = zero
+        buf[slot, buf.shape[1] - 1] = zero
+
+
+def run_forward(buf, slots, src_c, src_v, sp, hf, after_step, steps):
+    n_src = src_c.shape[0] // 3
+    for t in range(steps):
+        step_pass(buf, slots[t + 1], slots[t], slots[t + 2], sp, hf)
+        add_points(buf, slots[t + 2], src_c, src_v, t * n_src, n_src)
+        after_step(t, slots[t + 2])
+
+
+def forward_kernel(src_c, src_v, rec_c, u0, um1, sp, hf, final_out, synth_out, buf):
+    zero_edges(buf)
+    load_padded(buf, 0, um1)
+    load_padded(buf, 1, u0)
+    nrec = rec_c.shape[0] // 3
+    depth = buf.shape[-1]
+    sub = lax.broadcasted_iota(jnp.int32, (8, depth), 0)
+    lane = lax.broadcasted_iota(jnp.int32, (8, depth), 1)
+
+    def after_step(t, slot):
+        def body(r, carry):
+            x = rec_c[3 * r]
+            y = rec_c[3 * r + 1]
+            z = rec_c[3 * r + 2]
+            y8 = pl.multiple_of((y // 8) * 8, 8)
+            tile = buf[slot, x + 1, pl.ds(y8, 8), :]
+            hit = (sub == y - y8) & (lane == z)
+            synth_out[t * nrec + r] = jnp.sum(jnp.where(hit, tile, 0.0), axis=0, keepdims=True)
+            return carry
+
+        lax.fori_loop(0, nrec, body, 0)
+
+    slots = [0, 1, 2, 0, 1, 2]
+    run_forward(buf, slots, src_c, src_v, sp, hf, after_step, STEPS)
+    rows = sp.shape[0]
+    cross = final_out.shape[1]
+    lo = (buf.shape[2] - cross) // 2
+    last = slots[STEPS + 1]
+
+    def body(i, carry):
+        x0 = pl.multiple_of(i * CX, CX)
+        final_out[pl.ds(x0, CX)] = buf[last, pl.ds(x0 + 1, CX), lo : lo + cross]
+        return carry
+
+    lax.fori_loop(0, rows // CX, body, 0)
+
+
+def adjoint_kernel(
+    src_c, src_v, inj_c, inj_v, u0, um1, lam5, lam6, sp, hf, gs_out, ga_out, waves, lams, img_h, img_v
+):
+    zero_edges(waves)
+    zero_edges(lams)
+    load_padded(waves, 0, um1)
+    load_padded(waves, 1, u0)
+    run_forward(waves, [0, 1, 2, 3, 4], src_c, src_v, sp, hf, lambda t, slot: None, STEPS - 1)
+    load_padded(lams, 0, lam6)
+    load_padded(lams, 1, lam5)
+    rows = sp.shape[0]
+    n_inj = inj_c.shape[0] // 3
+    order = [0, 1, 2, 0, 1, 2]
+    for k in range(STEPS):
+        t = STEPS - 1 - k
+        later, now, new = order[k], order[k + 1], order[k + 2]
+        step_pass(lams, now, later, new, sp, hf)
+        add_points(lams, new, inj_c, inj_v, t * n_inj, n_inj)
+        wave = t + 1
+
+        def body(i, carry, new=new, wave=wave, first=(k == 0)):
+            x0 = pl.multiple_of(i * CX, CX)
+            c = waves[wave, pl.ds(x0 + 1, CX)]
+            horizontal, vertical = stencil(
+                c, waves[wave, pl.ds(x0 + 2, CX)], waves[wave, pl.ds(x0, CX)]
+            )
+            earlier = lams[new, pl.ds(x0 + 1, CX)]
+            if first:
+                img_h[pl.ds(x0, CX)] = earlier * horizontal
+                img_v[pl.ds(x0, CX)] = earlier * vertical
+            else:
+                img_h[pl.ds(x0, CX)] = img_h[pl.ds(x0, CX)] + earlier * horizontal
+                img_v[pl.ds(x0, CX)] = img_v[pl.ds(x0, CX)] + earlier * vertical
+            return carry
+
+        lax.fori_loop(0, rows // CX, body, 0)
+
+    def body(i, carry):
+        x0 = pl.multiple_of(i * CX, CX)
+        h = img_h[pl.ds(x0, CX)]
+        gs_out[pl.ds(x0, CX)] = hf[pl.ds(x0, CX)] * h + img_v[pl.ds(x0, CX)]
+        ga_out[pl.ds(x0, CX)] = 2.0 * sp[pl.ds(x0, CX)] * h
+        return carry
+
+    lax.fori_loop(0, rows // CX, body, 0)
+
+
+SMEM = pl.BlockSpec(memory_space=pltpu.SMEM)
+VMEM = pl.BlockSpec(memory_space=pltpu.VMEM)
+PARAMS = pltpu.CompilerParams(vmem_limit_bytes=62 * 1024 * 1024)
+
+
+def forward_call(src_c, src_v, rec_c, u0, um1, sp, hf):
+    rows, wide, depth = u0.shape
+    nrec = rec_c.shape[0] // 3
+    cross = wide - 2 * MARGIN
+    return pl.pallas_call(
+        forward_kernel,
+        out_shape=(
+            jax.ShapeDtypeStruct((rows, cross, depth), jnp.float32),
+            jax.ShapeDtypeStruct((STEPS * nrec, 1, depth), jnp.float32),
+        ),
+        in_specs=[SMEM, SMEM, SMEM] + [VMEM] * 4,
+        out_specs=(VMEM, VMEM),
+        scratch_shapes=[pltpu.VMEM((3, rows + 2, wide, depth), jnp.float32)],
+        compiler_params=PARAMS,
+        cost_estimate=pl.CostEstimate(
+            flops=STEPS * 20 * rows * wide * depth,
+            bytes_accessed=5 * rows * wide * depth * 4,
+            transcendentals=0,
+        ),
+    )(src_c, src_v, rec_c, u0, um1, sp, hf)
+
+
+def adjoint_call(src_c, src_v, inj_c, inj_v, u0, um1, lam5, lam6, sp, hf):
+    rows, wide, depth = u0.shape
+    field = jax.ShapeDtypeStruct((rows, wide, depth), jnp.float32)
+    return pl.pallas_call(
+        adjoint_kernel,
+        out_shape=(field, field),
+        in_specs=[SMEM] * 4 + [VMEM] * 6,
+        out_specs=(VMEM, VMEM),
+        scratch_shapes=[
+            pltpu.VMEM((STEPS + 1, rows + 2, wide, depth), jnp.float32),
+            pltpu.VMEM((3, rows + 2, wide, depth), jnp.float32),
+            pltpu.VMEM((rows, wide, depth), jnp.float32),
+            pltpu.VMEM((rows, wide, depth), jnp.float32),
+        ],
+        compiler_params=PARAMS,
+        cost_estimate=pl.CostEstimate(
+            flops=STEPS * 70 * rows * wide * depth,
+            bytes_accessed=8 * rows * wide * depth * 4,
+            transcendentals=0,
+        ),
+    )(src_c, src_v, inj_c, inj_v, u0, um1, lam5, lam6, sp, hf)
 
 
 def shards(
@@ -87,6 +299,7 @@
     owned = speed_blocks.shape[0]
     nrec = receiver_cell.shape[1]
 
+    wide_y = cross + 2 * MARGIN
     info = jnp.concatenate(
         [
             source_cell.astype(jnp.float32),
@@ -172,38 +385,25 @@
         )
     ]
 
-    previous, current, later_adjoint, adjoint = wide_fields[1], wide_fields[0], wide_fields[3], wide_fields[2]
-    waves = []
-    misfits = []
-    for time_step in range(STEPS):
-        horizontal, vertical = curvatures(current)
-        advanced = 2.0 * current - previous + speeds * (hfactor * horizontal + vertical)
-        advanced = add_at(advanced, sx, sy, sz, wav_all[time_step])
-        synthetic = advanced[rx_own, ry_own, rz_own]
-        misfits.append(synthetic - observed[0, time_step])
-        waves.append(current)
-        previous, current = current, advanced
-    final_wave = current[:, MARGIN : MARGIN + cross]
-
-    misfit_own = jnp.stack(misfits)
+    u_now, u_before, lam_now, lam_later = wide_fields
+    valid_src = (sy >= 0) & (sy < wide_y)
+    src_coords = jnp.stack([sx, jnp.where(valid_src, sy, 0), sz], axis=1).reshape(-1)
+    src_vals = jnp.where(valid_src[None, :], wav_all, 0.0).reshape(-1)
+    rec_coords = jnp.stack([rx_own, ry_own, rz_own], axis=1).reshape(-1)
+    final_wide, synth_rows = forward_call(
+        src_coords, src_vals, rec_coords, u_now, u_before, speeds, hfactor
+    )
+    final_wave = final_wide
+    synthetic = jnp.sum(synth_rows, axis=-1).reshape(STEPS, nrec)
+    misfit_own = synthetic - observed[0]
     mis_below, mis_above = exchange(misfit_own, misfit_own, count)
-
-    image_horizontal = jnp.zeros_like(current)
-    image_vertical = jnp.zeros_like(current)
-    for time_step in range(STEPS - 1, -1, -1):
-        horizontal, vertical = curvatures(adjoint)
-        earlier = 2.0 * adjoint - later_adjoint + speeds * (hfactor * horizontal + vertical)
-        injected = jnp.concatenate(
-            [misfit_own[time_step], mis_below[time_step], mis_above[time_step]]
-        )
-        earlier = add_at(earlier, rx, ry, rz, injected)
-        wave_horizontal, wave_vertical = curvatures(waves[time_step])
-        image_horizontal = image_horizontal + earlier * wave_horizontal
-        image_vertical = image_vertical + earlier * wave_vertical
-        later_adjoint, adjoint = adjoint, earlier
-
-    gradient_speed = hfactor * image_horizontal + image_vertical
-    gradient_aniso = 2.0 * speeds * image_horizontal
+    valid_rec = (ry >= 0) & (ry < wide_y)
+    inj_coords = jnp.stack([rx, jnp.where(valid_rec, ry, 0), rz], axis=1).reshape(-1)
+    injected = jnp.concatenate([misfit_own, mis_below, mis_above], axis=1)
+    inj_vals = jnp.where(valid_rec[None, :], injected, 0.0).reshape(-1)
+    gradient_speed, gradient_aniso = adjoint_call(
+        src_coords, src_vals, inj_coords, inj_vals, u_now, u_before, lam_now, lam_later, speeds, hfactor
+    )
 
     position = (me + SPLIT // 2) % SPLIT
     has_below = jnp.logical_and(position > 0, me > 0).astype(jnp.float32)

time: 915 us -> 469 us (0.51); the launches traced: 898 us -> 467 us
  other arithmetic: 556 us -> 23.5 us
  Pallas kernels: 0 us -> 131 us
  waiting for transfers between devices: 192 us -> 89.6 us
  blocking collectives: 10.2 us -> 106 us
  starting transfers between devices: 34.5 us -> 24.7 us
  local copies, waits for them, and re-layouts: 83.6 us -> 74.2 us
    scatter-add x8 -> x0, other arithmetic: 431 us -> none  [add_at(): return field.at[xs, ys, zs].add(values, mode='drop')]
    pallas_call x0 -> x2, Pallas kernels: none -> 131 us  [the longest x1 92.5 us: adjoint_call(): pl.pallas_call(adjoint_kernel, out_shape=(field, field), in_specs=[SMEM]...]
    all_to_all x0 -> x1, blocking collectives: none -> 96 us  [shards(): lax.all_to_all(returning.reshape(count, capacity, 2 * row_len), 'shot', s...]
    all_to_all x1 -> x0, waiting for transfers between devices: 91.4 us -> none  [shards(): lax.all_to_all(returning.reshape(count, capacity, 2 * row_len), 'shot', s...]
    add x7 -> x3, other arithmetic: 85.6 us -> 3.83 us  [the longest x1 3.21 us: shards(): 1.0 + 2.0 * widen(aniso_own, model_below[:, HALO:], model_above[:, HALO:])]
    another operation x3 -> x1, other arithmetic: 26.5 us -> 1.86 us  [shards(): grads = jnp.stack([gradient_speed, gradient_aniso])]
    gather x4 -> x0, local copies, waits for them, and re-layouts: 14.6 us -> none  [shards(): synthetic = advanced[rx_own, ry_own, rz_own]]
    all_to_all x1 -> x0, starting transfers between devices: 9.67 us -> none  [shards(): lax.all_to_all(returning.reshape(count, capacity, 2 * row_len), 'shot', s...]
  transfers between devices with their start and end apart: 8 -> 7, of which waited for: 4 -> 1; matrix products, arithmetic and copies ran while one was open for 6% -> 13% of each run, Pallas kernels for 0% -> 0%
where the time goes in v1:
time: 469 us; the launch traced here: 467 us
  Pallas kernels  131 us (28%)
  blocking collectives  106 us (23%)
  waiting for transfers between devices  89.6 us (19%)
  local copies, waits for them, and re-layouts  74.2 us (16%)
  starting transfers between devices  24.7 us (5%)
  other arithmetic  23.5 us (5%)
  matrix products  14.3 us (3%)
    all_to_all x1, blocking collectives, shards(): lax.all_to_all(returning.reshape(count, capacity, 2 * row_len), 'shot', s...  96 us
    pallas_call x1, Pallas kernels, adjoint_call(): pl.pallas_call(adjoint_kernel, out_shape=(field, field), in_specs=[SMEM]...  92.5 us
    ppermute x3, waiting for transfers between devices, exchange(): from_above = lax.ppermute(bottom, 'shot', down)  89.6 us
    pallas_call x1, Pallas kernels, forward_call(): pl.pallas_call(forward_kernel, out_shape=(jax.ShapeDtypeStruct((rows, cro...  38.5 us
    concatenate x6, local copies, waits for them, and re-layouts, widen(): return jnp.concatenate([zeros, below, own, above, zeros], axis=1)  35.6 us
    unnamed x76, local copies, waits for them, and re-layouts  20.4 us
    ppermute x3, starting transfers between devices, exchange(): from_below = lax.ppermute(top, 'shot', up)  11.1 us
    all_to_all x1, blocking collectives, shards(): lax.all_to_all(requests.reshape(count, capacity), 'shot', split_axis=0, c...  10.2 us
  transfers between devices with their start and end apart: 7, of which 1 were waited for; matrix products, arithmetic and copies ran while one was open for 13% of the time, Pallas kernels for 0%

profile of v1, /device:TPU:13, one launch (start us, length us, event | category | flops | bytes accessed | tf_op | source)
XLA Modules:
  0.0 466.9 jit_solution(10144474235476884019)
XLA Ops:
  0.6 0.7 fusion.54
  1.5 0.8 select_reduce_fusion
  2.4 1.2 fusion.71
  3.6 1.1 scatter_custom_fusion
  4.8 10.2 %all_to_all.19 = s32[16,1,16]{2,1,0:T(1,128)S(1)} all-to-all(s32[16,1,16]{2,1,0:T(1,128)S(1)} %all_to_all.12), channel_id=1, replica_groups=mesh['groups'=2,'shot'=16] {'shot'}, dimensions={0} | all-to-all | bytes 2048 | tf_op jit(solution)/shard_map/all_to_all | solution.py:322
  15.4 0.7 reduce.4
  16.2 5.1 %fusion.39 = f32[256,4096]{1,0:T(8,128)} fusion(f32[64,2048]{1,0:T(8,128)} %param.13, f32[64,2048]{1,0:T(8,128)} %param.12, s32[256]{0:T(256)S(1)} %eq.90), kind=kOutput, calls=%fused_computation.59 | convolution fusion | flops 805584896 | bytes 5243904 | tf_op jit(solution)/shard_map/dot_general | solution.py:328
  21.3 7.1 %all-to-all-start.1 = ((f32[16,16,4096]{2,1,0:T(8,128)}), f32[16,16,4096]{2,1,0:T(8,128)}, u32[]{:S(2)}, u32[]{:S(2)}) async-start(f32[16,16,4096]{2,1,0:T(8,128)} %bitcast.105), calls=%async_computation.1 | async-start | bytes 8388608 | tf_op jit(solution)/shard_map/all_to_all | solution.py:329
  29.3 1.0 copy_dynamic-update-slice_fusion.3
  30.4 0.8 copy_dynamic-update-slice_fusion.6
  31.3 0.8 copy_dynamic-update-slice_fusion.5
  32.2 0.8 copy_dynamic-update-slice_fusion.4
  33.0 0.8 copy_dynamic-update-slice_fusion.2
  33.8 0.8 copy_dynamic-update-slice_fusion.1
  34.6 0.8 copy_dynamic-update-slice_fusion
  35.3 0.7 fusion.48
  36.1 2.3 collective-permute-start.1
  38.3 4.2 collective-permute-start
  42.8 0.8 reshape.625.rec_c
  44.8 0.7 slice_bitcast_fusion.7
  46.1 89.6 %collective-permute-done.1 = f32[128,21,128]{2,0,1:T(8,128)S(1)} collective-permute-done((f32[128,21,128]{2,0,1:T(8,128)}, f32[128,21,128]{2,0,1:T(8,128)S(1)}, u32[]{:S(2)}, u32[]{:S(2)}) %collective-permute-start.1) | collective-permute-done | bytes 1376288 | tf_op jit(solution)/shard_map/ppermute | solution.py:30
  138.5 0.6 reshape.624.src_c
  140.2 0.8 fusion.73
  141.2 1.0 fusion.72
  142.2 1.0 copy.61
  143.2 1.0 copy.62
  144.3 1.0 copy.63
  145.5 3.9 fusion.43
  150.3 1.0 copy.37
  151.3 2.4 collective-permute-start.2
  153.9 1.0 copy.39
  154.9 2.3 collective-permute-start.3
  157.5 0.8 reshape.630.inj_c
  158.3 2.0 copy.68
  160.3 2.0 copy.69
  162.3 1.0 copy.70
  163.3 1.0 copy.71
  164.3 6.2 %concatenate.119.u0 = f32[128,32,128]{2,1,0:T(8,128)} concatenate(f32[128,3,128]{2,1,0:T(4,128)S(1)} %broadcast.563, f32[128,5,128]{2,1,0:T(8,128)S(1)} %copy.60, f32[128,16,128]{2,1,0:T(8,128)} %param.16, f32[128,5,128]{2,1,0:T(8,128)} %copy.61, f32[128,3,128]{2,1,0:T(4,128)S(1)} %broadcast.563), dimensions={1} | concatenate | bytes 4194304 | tf_op jit(solution)/shard_map/concatenate | solution.py:38
  170.6 7.1 %concatenate.120.um1 = f32[128,32,128]{2,1,0:T(8,128)} concatenate(f32[128,3,128]{2,1,0:T(4,128)S(1)} %broadcast.563, f32[128,5,128]{2,1,0:T(8,128)} %copy.62, f32[128,16,128]{2,1,0:T(8,128)} %param.17, f32[128,5,128]{2,1,0:T(8,128)} %copy.63, f32[128,3,128]{2,1,0:T(4,128)S(1)} %broadcast.563), dimensions={1} | concatenate | bytes 4194304 | tf_op jit(solution)/shard_map/concatenate | solution.py:38
  177.7 6.2 %concatenate.135.lam5 = f32[128,32,128]{2,1,0:T(8,128)} concatenate(f32[128,3,128]{2,1,0:T(4,128)S(1)} %broadcast.563, f32[128,5,128]{2,1,0:T(8,128)S(1)} %copy-done.10, f32[128,16,128]{2,1,0:T(8,128)} %param.18, f32[128,5,128]{2,1,0:T(8,128)} %copy.69, f32[128,3,128]{2,1,0:T(4,128)S(1)} %broadcast.563), dimensions={1} | concatenate | bytes 4194304 | tf_op jit(solution)/shard_map/concatenate | solution.py:38
  183.9 7.1 %concatenate.136.lam6 = f32[128,32,128]{2,1,0:T(8,128)} concatenate(f32[128,3,128]{2,1,0:T(4,128)S(1)} %broadcast.563, f32[128,5,128]{2,1,0:T(8,128)} %copy.70, f32[128,16,128]{2,1,0:T(8,128)} %param.19, f32[128,5,128]{2,1,0:T(8,128)} %copy.71, f32[128,3,128]{2,1,0:T(4,128)S(1)} %broadcast.563), dimensions={1} | concatenate | bytes 4194304 | tf_op jit(solution)/shard_map/concatenate | solution.py:38
  191.0 1.1 fusion.81
  192.4 1.1 fusion.80
  193.5 1.0 copy.65
  194.5 1.0 copy.66
  195.5 1.0 copy.67
  196.5 5.4 %concatenate.125 = f32[128,32,128]{2,1,0:T(8,128)} concatenate(f32[128,3,128]{2,1,0:T(4,128)S(1)} %broadcast.563, f32[128,5,128]{2,1,0:T(8,128)} %copy.66, f32[128,16,128]{2,1,0:T(8,128)S(1)} %bitcast.111, f32[128,5,128]{2,1,0:T(8,128)} %copy.67, f32[128,3,128]{2,1,0:T(4,128)S(1)} %broadcast.563), dimensions={1} | concatenate | bytes 4194304 | tf_op jit(solution)/shard_map/concatenate | solution.py:38
  201.9 3.2 multiply_add_fusion.hf
  205.1 3.6 concatenate.124.sp
  208.7 38.5 %shard_map.131 = (f32[128,16,128]{2,1,0:T(8,128)}, f32[1024,1,128]{2,1,0:T(1,128)}) custom-call(s32[9]{0:T(128)} %reshape.624.src_c, f32[12]{0:T(128)} %select_n.242.src_v, s32[768]{0:T(1024)} %reshape.625.rec_c, f32[128,32,128]{2,1,0:T(8,128)} %concatenate.119.u0, f32[128,32,128]{2,1,0:T(8,128)} %concatenate.120.um1, f32[128,32,128]{2,1,0:T(8,128)} %concatenate.124.sp, ...), custom_call_target="tpu_custom_call" | custom-call | flops 41943040 | bytes 10485760 | tf_op jit(solution)/shard_map/pallas_call | solution.py:238
  247.2 2.8 reduce_sum.22
  250.0 1.9 collective-permute-start.5
  252.0 4.5 collective-permute-start.4
  256.7 4.5 fusion.17
  261.2 0.6 select_n.264.inj_v
  261.8 92.5 %shard_map.132 = (f32[128,32,128]{2,1,0:T(8,128)}, f32[128,32,128]{2,1,0:T(8,128)}) custom-call(s32[9]{0:T(128)} %reshape.624.src_c, f32[12]{0:T(128)} %select_n.242.src_v, s32[2304]{0:T(1024)} %reshape.630.inj_c, f32[3072]{0:T(1024)} %select_n.264.inj_v, f32[128,32,128]{2,1,0:T(8,128)} %concatenate.119.u0, f32[128,32,128]{2,1,0:T(8,128)} %concatenate.120.um1, ...), custom_call_target="tpu_custom_call" | custom-call | flops 146800640 | bytes 16777216 | tf_op jit(solution)/shard_map/pallas_call | solution.py:259
  354.3 1.9 fusion.14
  356.5 0.6 copy-done.1
  357.8 4.0 fusion.6
  361.8 1.9 copy.48
  363.7 3.5 fusion.44
  367.2 96.0 %all_to_all.20 = f32[16,16,4096]{2,1,0:T(8,128)S(1)} all-to-all(f32[16,16,4096]{2,1,0:T(8,128)S(1)} %fusion.44), channel_id=1, replica_groups=mesh['groups'=2,'shot'=16] {'shot'}, dimensions={0} | all-to-all | bytes 8388608 | tf_op jit(solution)/shard_map/all_to_all | solution.py:448
  463.2 1.8 convolution_multiply_fusion
  465.0 1.9 reshape.634
  (114 shorter events, 8.5 us)
Async XLA Ops:
  16.2 5.1 %copy-start.14 = (s32[256]{0:T(256)}, s32[256]{0:T(256)S(1)}, u32[]{:S(2)}) copy-start(s32[256]{0:T(256)S(1)} %eq.90) | copy-start | bytes 3076
  21.3 7.2 %copy-start.13 = (s32[1,256]{1,0:T(1,128)S(1)}, s32[1,256]{1,0:T(1,128)}, u32[]{:S(2)}) copy-start(s32[1,256]{1,0:T(1,128)} %param.22) | copy-start | bytes 3076
  21.3 7.9 %copy-start.6 = (f32[128,16,128]{2,1,0:T(8,128)S(1)}, f32[128,16,128]{2,1,0:T(8,128)}, u32[]{:S(2)}) copy-start(f32[128,16,128]{2,1,0:T(8,128)} %param.16) | copy-start | bytes 3145732
  21.3 124.2 %all-to-all-start.1 = ((f32[16,16,4096]{2,1,0:T(8,128)}), f32[16,16,4096]{2,1,0:T(8,128)}, u32[]{:S(2)}, u32[]{:S(2)}) async-start(f32[16,16,4096]{2,1,0:T(8,128)} %bitcast.105), calls=%async_computation.1 | async-start | bytes 8388608 | tf_op jit(solution)/shard_map/all_to_all | solution.py:329
  28.4 1.9 copy-start.7
  29.3 1.9 copy-start.8
  30.4 1.7 copy-start.9
  32.2 3.1 copy-start.26
  36.1 99.6 %collective-permute-start.1 = (f32[128,21,128]{2,0,1:T(8,128)}, f32[128,21,128]{2,0,1:T(8,128)S(1)}, u32[]{:S(2)}, u32[]{:S(2)}) collective-permute-start(f32[128,21,128]{2,0,1:T(8,128)} %get-tuple-element.51), channel_id=1, source_target_pairs={{1,0},{2,1},{3,2},{5,4},{6,5},{7,6},{8,7},{9,8},{10,9},{11,10},{13... | collective-permute-start | bytes 4128776 | tf_op jit(solution)/shard_map/ppermute | solution.py:30
  38.3 98.6 %collective-permute-start = (f32[128,21,128]{2,0,1:T(8,128)}, f32[128,21,128]{2,0,1:T(8,128)S(1)}, u32[]{:S(2)}, u32[]{:S(2)}) collective-permute-start(f32[128,21,128]{2,0,1:T(8,128)} %get-tuple-element.50), channel_id=1, source_target_pairs={{0,1},{1,2},{2,3},{4,5},{5,6},{6,7},{7,8},{8,9},{9,10},{10,11},{12... | collective-permute-start | bytes 4128776 | tf_op jit(solution)/shard_map/ppermute | solution.py:29
  141.2 4.3 copy-start.16
  150.1 3.6 copy-start.20
  151.3 5.9 %copy-start.19 = (s32[256]{0:T(256)S(1)}, s32[256]{0:T(256)}, u32[]{:S(2)}) copy-start(s32[256]{0:T(256)} %get-tuple-element.52) | copy-start | bytes 3076
  151.3 5.9 %copy-start.22 = (s32[256]{0:T(256)S(1)}, s32[256]{0:T(256)}, u32[]{:S(2)}) copy-start(s32[256]{0:T(256)} %get-tuple-element.53) | copy-start | bytes 3076
  151.3 39.7 %collective-permute-start.2 = (f32[128,10,128]{2,0,1:T(8,128)}, f32[128,10,128]{2,0,1:T(8,128)}, u32[]{:S(2)}, u32[]{:S(2)}) collective-permute-start(f32[128,10,128]{2,0,1:T(8,128)} %copy.37), channel_id=1, source_target_pairs={{0,1},{1,2},{2,3},{4,5},{5,6},{6,7},{7,8},{8,9},{9,10},{10,11},{12... | collective-permute-start | bytes 1966088 | tf_op jit(solution)/shard_map/ppermute | solution.py:29
  154.9 37.5 %collective-permute-start.3 = (f32[128,10,128]{2,0,1:T(8,128)}, f32[128,10,128]{2,0,1:T(8,128)}, u32[]{:S(2)}, u32[]{:S(2)}) collective-permute-start(f32[128,10,128]{2,0,1:T(8,128)} %copy.39), channel_id=1, source_target_pairs={{1,0},{2,1},{3,2},{5,4},{6,5},{7,6},{8,7},{9,8},{10,9},{11,10},{13... | collective-permute-start | bytes 1966088 | tf_op jit(solution)/shard_map/ppermute | solution.py:30
  158.3 5.0 %copy-start.11 = (f32[128,5,128]{2,0,1:T(8,128)S(1)}, f32[128,5,128]{2,0,1:T(8,128)}, u32[]{:S(2)}) copy-start(f32[128,5,128]{2,0,1:T(8,128)} %get-tuple-element.18) | copy-start | bytes 983044
  170.6 7.1 %copy-start.10 = (f32[128,5,128]{2,1,0:T(8,128)S(1)}, f32[128,5,128]{2,1,0:T(8,128)}, u32[]{:S(2)}) copy-start(f32[128,5,128]{2,1,0:T(8,128)} %copy.68) | copy-start | bytes 983044
  183.9 7.1 %copy-start.21 = (s32[1,256]{1,0:T(1,128)S(1)}, s32[1,256]{1,0:T(1,128)}, u32[]{:S(2)}) copy-start(s32[1,256]{1,0:T(1,128)} %fusion.62) | copy-start | bytes 3076
  201.9 3.2 copy-start.2
  208.7 41.3 %copy-start.18 = (f32[1,4,256]{2,1,0:T(4,128)S(1)}, f32[1,4,256]{2,1,0:T(4,128)}, u32[]{:S(2)}) copy-start(f32[1,4,256]{2,1,0:T(4,128)} %param.23) | copy-start | bytes 12292
  208.7 47.8 %copy-start.25 = (f32[16]{0:T(128)S(1)}, f32[16]{0:T(128)}, u32[]{:S(2)}) copy-start(f32[16]{0:T(128)} %get-tuple-element.60) | copy-start | bytes 196
  208.7 48.0 %copy-start.23 = (f32[16]{0:T(128)S(1)}, f32[16]{0:T(128)}, u32[]{:S(2)}) copy-start(f32[16]{0:T(128)} %get-tuple-element.58) | copy-start | bytes 196
  208.7 48.0 %copy-start.24 = (f32[16]{0:T(128)S(1)}, f32[16]{0:T(128)}, u32[]{:S(2)}) copy-start(f32[16]{0:T(128)} %get-tuple-element.59) | copy-start | bytes 196
  250.0 11.2 %collective-permute-start.5 = (f32[4,256]{1,0:T(4,128)S(1)}, f32[4,256]{1,0:T(4,128)S(1)}, u32[]{:S(2)}, u32[]{:S(2)}) collective-permute-start(f32[4,256]{1,0:T(4,128)S(1)} %bitcast_subtract_fusion), channel_id=1, source_target_pairs={{1,0},{2,1},{3,2},{5,4},{6,5},{7,6},{8,7},{9,8},{10,9},{11,10},{13... | collective-permute-start | bytes 12296 | tf_op jit(solution)/shard_map/ppermute | solution.py:30
  252.0 9.2 %collective-permute-start.4 = (f32[4,256]{1,0:T(4,128)S(1)}, f32[4,256]{1,0:T(4,128)S(1)}, u32[]{:S(2)}, u32[]{:S(2)}) collective-permute-start(f32[4,256]{1,0:T(4,128)S(1)} %bitcast_subtract_fusion), channel_id=1, source_target_pairs={{0,1},{1,2},{2,3},{4,5},{5,6},{6,7},{7,8},{8,9},{9,10},{10,11},{12... | collective-permute-start | bytes 12296 | tf_op jit(solution)/shard_map/ppermute | solution.py:29
  261.8 94.4 %copy-start.5 = (f32[128,16,128]{2,1,0:T(8,128)S(1)}, f32[128,16,128]{2,1,0:T(8,128)}, u32[]{:S(2)}) copy-start(f32[128,16,128]{2,1,0:T(8,128)} %get-tuple-element.14) | copy-start | bytes 3145732
  354.3 2.2 copy-start
  354.3 2.9 copy-start.1
  354.3 3.1 copy-start.3
  354.3 3.4 copy-start.4
  361.7 1.9 copy-start.12
  361.8 1.9 copy-start.17
  367.2 96.0 %copy-start.15 = (s32[256]{0:T(256)S(1)}, s32[256]{0:T(256)}, u32[]{:S(2)}) copy-start(s32[256]{0:T(256)} %copy-done.14) | copy-start | bytes 3076

commit v2 on v1

--- a/solution.py
+++ b/solution.py
@@ -81,8 +81,9 @@
     return horizontal, vertical
 
 
-def step_pass(buf, cur, prev, new, sp, hf):
-    rows = sp.shape[0]
+def step_pass(buf, cur, prev, new, model):
+    rows = model.shape[1]
+    sp, hf = model.at[0], model.at[1]
 
     def body(i, carry):
         x0 = pl.multiple_of(i * CX, CX)
@@ -97,12 +98,12 @@
     lax.fori_loop(0, rows // CX, body, 0)
 
 
-def add_points(buf, slot, coords, vals, base, count):
+def add_points(buf, slot, coords, vals, base, first, count, checked):
     depth = buf.shape[-1]
     sub = lax.broadcasted_iota(jnp.int32, (8, depth), 0)
     lane = lax.broadcasted_iota(jnp.int32, (8, depth), 1)
 
-    def body(k, carry):
+    def one(k):
         x = coords[3 * k]
         y = coords[3 * k + 1]
         z = coords[3 * k + 2]
@@ -111,17 +112,43 @@
         tile = buf[slot, x + 1, pl.ds(y8, 8), :]
         hit = (sub == y - y8) & (lane == z)
         buf[slot, x + 1, pl.ds(y8, 8), :] = tile + jnp.where(hit, val, 0.0)
+
+    def body(k, carry):
+        if checked:
+            pl.when(coords[3 * k + 1] > 0)(lambda: one(k))
+        else:
+            one(k)
         return carry
 
-    lax.fori_loop(0, count, body, 0)
-
-
-def load_padded(buf, slot, field):
-    rows = field.shape[0]
+    lax.fori_loop(first, first + count, body, 0, unroll=8)
+
+
+def load_padded(buf, slot, own, below, above, k, pad=1):
+    rows, cross, depth = own.shape
+    gap = MARGIN - HALO
+    zeros = jnp.zeros((CX, gap, depth), jnp.float32)
 
     def body(i, carry):
         x0 = pl.multiple_of(i * CX, CX)
-        buf[slot, pl.ds(x0 + 1, CX)] = field[pl.ds(x0, CX)]
+        xs = pl.ds(x0 + pad, CX)
+        buf[slot, xs, 0:gap] = zeros
+        buf[slot, xs, gap:MARGIN] = below[pl.ds(x0, CX), k * HALO : (k + 1) * HALO]
+        buf[slot, xs, MARGIN : MARGIN + cross] = own[pl.ds(x0, CX)]
+        buf[slot, xs, MARGIN + cross : MARGIN + cross + HALO] = above[pl.ds(x0, CX), k * HALO : (k + 1) * HALO]
+        buf[slot, xs, MARGIN + cross + HALO :] = zeros
+        return carry
+
+    lax.fori_loop(0, rows // CX, body, 0)
+
+
+def load_model(model, sp_own, an_own, m_lo, m_hi):
+    load_padded(model, 0, sp_own, m_lo, m_hi, 0, pad=0)
+    load_padded(model, 1, an_own, m_lo, m_hi, 1, pad=0)
+    rows = sp_own.shape[0]
+
+    def body(i, carry):
+        x0 = pl.multiple_of(i * CX, CX)
+        model[1, pl.ds(x0, CX)] = 1.0 + 2.0 * model[1, pl.ds(x0, CX)]
         return carry
 
     lax.fori_loop(0, rows // CX, body, 0)
@@ -134,18 +161,21 @@
         buf[slot, buf.shape[1] - 1] = zero
 
 
-def run_forward(buf, slots, src_c, src_v, sp, hf, after_step, steps):
+def run_forward(buf, slots, src_c, src_v, model, after_step, steps):
     n_src = src_c.shape[0] // 3
     for t in range(steps):
-        step_pass(buf, slots[t + 1], slots[t], slots[t + 2], sp, hf)
-        add_points(buf, slots[t + 2], src_c, src_v, t * n_src, n_src)
+        step_pass(buf, slots[t + 1], slots[t], slots[t + 2], model)
+        add_points(buf, slots[t + 2], src_c, src_v, t * n_src, 0, n_src, False)
         after_step(t, slots[t + 2])
 
 
-def forward_kernel(src_c, src_v, rec_c, u0, um1, sp, hf, final_out, synth_out, buf):
+def forward_kernel(
+    src_c, src_v, rec_c, u0, um1, sp_own, an_own, lo, hi, m_lo, m_hi, final_out, synth_out, buf, model
+):
     zero_edges(buf)
-    load_padded(buf, 0, um1)
-    load_padded(buf, 1, u0)
+    load_padded(buf, 0, um1, lo, hi, 1)
+    load_padded(buf, 1, u0, lo, hi, 0)
+    load_model(model, sp_own, an_own, m_lo, m_hi)
     nrec = rec_c.shape[0] // 3
     depth = buf.shape[-1]
     sub = lax.broadcasted_iota(jnp.int32, (8, depth), 0)
@@ -162,11 +192,11 @@
             synth_out[t * nrec + r] = jnp.sum(jnp.where(hit, tile, 0.0), axis=0, keepdims=True)
             return carry
 
-        lax.fori_loop(0, nrec, body, 0)
+        lax.fori_loop(0, nrec, body, 0, unroll=8)
 
     slots = [0, 1, 2, 0, 1, 2]
-    run_forward(buf, slots, src_c, src_v, sp, hf, after_step, STEPS)
-    rows = sp.shape[0]
+    run_forward(buf, slots, src_c, src_v, model, after_step, STEPS)
+    rows = u0.shape[0]
     cross = final_out.shape[1]
     lo = (buf.shape[2] - cross) // 2
     last = slots[STEPS + 1]
@@ -180,23 +210,27 @@
 
 
 def adjoint_kernel(
-    src_c, src_v, inj_c, inj_v, u0, um1, lam5, lam6, sp, hf, gs_out, ga_out, waves, lams, img_h, img_v
+    src_c, src_v, inj_c, inj_v, u0, um1, lam5, lam6, sp_own, an_own, lo, hi, m_lo, m_hi,
+    gs_out, ga_out, waves, lams, img_h, img_v, model,
 ):
     zero_edges(waves)
     zero_edges(lams)
-    load_padded(waves, 0, um1)
-    load_padded(waves, 1, u0)
-    run_forward(waves, [0, 1, 2, 3, 4], src_c, src_v, sp, hf, lambda t, slot: None, STEPS - 1)
-    load_padded(lams, 0, lam6)
-    load_padded(lams, 1, lam5)
-    rows = sp.shape[0]
+    load_model(model, sp_own, an_own, m_lo, m_hi)
+    load_padded(waves, 0, um1, lo, hi, 1)
+    load_padded(waves, 1, u0, lo, hi, 0)
+    run_forward(waves, [0, 1, 2, 3, 4], src_c, src_v, model, lambda t, slot: None, STEPS - 1)
+    load_padded(lams, 0, lam6, lo, hi, 3)
+    load_padded(lams, 1, lam5, lo, hi, 2)
+    rows = u0.shape[0]
     n_inj = inj_c.shape[0] // 3
+    n_own = n_inj // 3
     order = [0, 1, 2, 0, 1, 2]
     for k in range(STEPS):
         t = STEPS - 1 - k
         later, now, new = order[k], order[k + 1], order[k + 2]
-        step_pass(lams, now, later, new, sp, hf)
-        add_points(lams, new, inj_c, inj_v, t * n_inj, n_inj)
+        step_pass(lams, now, later, new, model)
+        add_points(lams, new, inj_c, inj_v, t * n_inj, 0, n_own, False)
+        add_points(lams, new, inj_c, inj_v, t * n_inj, n_own, n_inj - n_own, True)
         wave = t + 1
 
         def body(i, carry, new=new, wave=wave, first=(k == 0)):
@@ -219,8 +253,8 @@
     def body(i, carry):
         x0 = pl.multiple_of(i * CX, CX)
         h = img_h[pl.ds(x0, CX)]
-        gs_out[pl.ds(x0, CX)] = hf[pl.ds(x0, CX)] * h + img_v[pl.ds(x0, CX)]
-        ga_out[pl.ds(x0, CX)] = 2.0 * sp[pl.ds(x0, CX)] * h
+        gs_out[pl.ds(x0, CX)] = model[1, pl.ds(x0, CX)] * h + img_v[pl.ds(x0, CX)]
+        ga_out[pl.ds(x0, CX)] = 2.0 * model[0, pl.ds(x0, CX)] * h
         return carry
 
     lax.fori_loop(0, rows // CX, body, 0)
@@ -231,49 +265,54 @@
 PARAMS = pltpu.CompilerParams(vmem_limit_bytes=62 * 1024 * 1024)
 
 
-def forward_call(src_c, src_v, rec_c, u0, um1, sp, hf):
-    rows, wide, depth = u0.shape
+def forward_call(src_c, src_v, rec_c, u0, um1, sp_own, an_own, lo, hi, m_lo, m_hi):
+    rows, cross, depth = u0.shape
+    wide = cross + 2 * MARGIN
     nrec = rec_c.shape[0] // 3
-    cross = wide - 2 * MARGIN
     return pl.pallas_call(
         forward_kernel,
         out_shape=(
             jax.ShapeDtypeStruct((rows, cross, depth), jnp.float32),
             jax.ShapeDtypeStruct((STEPS * nrec, 1, depth), jnp.float32),
         ),
-        in_specs=[SMEM, SMEM, SMEM] + [VMEM] * 4,
+        in_specs=[SMEM] * 3 + [VMEM] * 8,
         out_specs=(VMEM, VMEM),
-        scratch_shapes=[pltpu.VMEM((3, rows + 2, wide, depth), jnp.float32)],
+        scratch_shapes=[
+            pltpu.VMEM((3, rows + 2, wide, depth), jnp.float32),
+            pltpu.VMEM((2, rows, wide, depth), jnp.float32),
+        ],
         compiler_params=PARAMS,
         cost_estimate=pl.CostEstimate(
             flops=STEPS * 20 * rows * wide * depth,
-            bytes_accessed=5 * rows * wide * depth * 4,
+            bytes_accessed=6 * rows * cross * depth * 4,
             transcendentals=0,
         ),
-    )(src_c, src_v, rec_c, u0, um1, sp, hf)
-
-
-def adjoint_call(src_c, src_v, inj_c, inj_v, u0, um1, lam5, lam6, sp, hf):
-    rows, wide, depth = u0.shape
+    )(src_c, src_v, rec_c, u0, um1, sp_own, an_own, lo, hi, m_lo, m_hi)
+
+
+def adjoint_call(src_c, src_v, inj_c, inj_v, u0, um1, lam5, lam6, sp_own, an_own, lo, hi, m_lo, m_hi):
+    rows, cross, depth = u0.shape
+    wide = cross + 2 * MARGIN
     field = jax.ShapeDtypeStruct((rows, wide, depth), jnp.float32)
     return pl.pallas_call(
         adjoint_kernel,
         out_shape=(field, field),
-        in_specs=[SMEM] * 4 + [VMEM] * 6,
+        in_specs=[SMEM] * 4 + [VMEM] * 10,
         out_specs=(VMEM, VMEM),
         scratch_shapes=[
             pltpu.VMEM((STEPS + 1, rows + 2, wide, depth), jnp.float32),
             pltpu.VMEM((3, rows + 2, wide, depth), jnp.float32),
             pltpu.VMEM((rows, wide, depth), jnp.float32),
             pltpu.VMEM((rows, wide, depth), jnp.float32),
+            pltpu.VMEM((2, rows, wide, depth), jnp.float32),
         ],
         compiler_params=PARAMS,
         cost_estimate=pl.CostEstimate(
             flops=STEPS * 70 * rows * wide * depth,
-            bytes_accessed=8 * rows * wide * depth * 4,
+            bytes_accessed=10 * rows * cross * depth * 4,
             transcendentals=0,
         ),
-    )(src_c, src_v, inj_c, inj_v, u0, um1, lam5, lam6, sp, hf)
+    )(src_c, src_v, inj_c, inj_v, u0, um1, lam5, lam6, sp_own, an_own, lo, hi, m_lo, m_hi)
 
 
 def shards(
@@ -345,13 +384,6 @@
         jnp.concatenate([speed_own[:, :HALO], aniso_own[:, :HALO]], axis=1),
         count,
     )
-    speeds = widen(speed_own, model_below[:, :HALO], model_above[:, :HALO])
-    hfactor = 1.0 + 2.0 * widen(aniso_own, model_below[:, HALO:], model_above[:, HALO:])
-
-    def part(received, k):
-        return received[:, k * HALO : (k + 1) * HALO]
-
-    wide_fields = [widen(f, part(from_below, k), part(from_above, k)) for k, f in enumerate(fields)]
     info_below = from_below[:, 4 * HALO].reshape(-1)
     info_above = from_above[:, 4 * HALO].reshape(-1)
 
@@ -385,24 +417,28 @@
         )
     ]
 
-    u_now, u_before, lam_now, lam_later = wide_fields
     valid_src = (sy >= 0) & (sy < wide_y)
     src_coords = jnp.stack([sx, jnp.where(valid_src, sy, 0), sz], axis=1).reshape(-1)
     src_vals = jnp.where(valid_src[None, :], wav_all, 0.0).reshape(-1)
     rec_coords = jnp.stack([rx_own, ry_own, rz_own], axis=1).reshape(-1)
+    halos = (from_below, from_above, model_below, model_above)
     final_wide, synth_rows = forward_call(
-        src_coords, src_vals, rec_coords, u_now, u_before, speeds, hfactor
+        src_coords, src_vals, rec_coords, state_now, state_prev, speed_own, aniso_own, *halos
     )
     final_wave = final_wide
     synthetic = jnp.sum(synth_rows, axis=-1).reshape(STEPS, nrec)
     misfit_own = synthetic - observed[0]
     mis_below, mis_above = exchange(misfit_own, misfit_own, count)
-    valid_rec = (ry >= 0) & (ry < wide_y)
+    valid_rec = (ry >= MARGIN - HALO + 1) & (ry < MARGIN + cross + HALO - 1)
     inj_coords = jnp.stack([rx, jnp.where(valid_rec, ry, 0), rz], axis=1).reshape(-1)
     injected = jnp.concatenate([misfit_own, mis_below, mis_above], axis=1)
     inj_vals = jnp.where(valid_rec[None, :], injected, 0.0).reshape(-1)
     gradient_speed, gradient_aniso = adjoint_call(
-        src_coords, src_vals, inj_coords, inj_vals, u_now, u_before, lam_now, lam_later, speeds, hfactor
+        src_coords, src_vals, inj_coords, inj_vals, state_now, state_prev, adjoint_now, adjoint_prev,
+        speed_own, aniso_own, *halos
+    )
+    speeds = jnp.concatenate(
+        [model_below[:, HALO - 1 : HALO], speed_own, model_above[:, 0:1]], axis=1
     )
 
     position = (me + SPLIT // 2) % SPLIT
@@ -410,13 +446,11 @@
     has_above = jnp.logical_and(position < SPLIT - 1, me < count - 1).astype(jnp.float32)
     wide = speeds.shape[1]
     layer = lax.broadcasted_iota(jnp.int32, (1, wide, 1), 1)
-    exists = jnp.where(
-        layer < MARGIN, has_below, jnp.where(layer >= MARGIN + cross, has_above, 1.0)
-    )
+    exists = jnp.where(layer < 1, has_below, jnp.where(layer >= 1 + cross, has_above, 1.0))
     exists = jnp.broadcast_to(exists, speeds.shape)
 
-    lo, hi = MARGIN, MARGIN + cross
-    grads = jnp.stack([gradient_speed, gradient_aniso])
+    lo, hi = 1, 1 + cross
+    grads = jnp.stack([gradient_speed, gradient_aniso])[:, :, MARGIN - 1 : MARGIN + cross + 1]
     center_g = grads[:, :, lo:hi]
     center_s = speeds[:, lo:hi]
 

time: 469 us -> 406 us (0.87)
  local copies, waits for them, and re-layouts: 74.2 us -> 33.2 us
  Pallas kernels: 131 us -> 112 us
  other arithmetic: 23.5 us -> 16.9 us
    concatenate x6 -> x0, local copies, waits for them, and re-layouts: 35.6 us -> none  [widen(): return jnp.concatenate([zeros, below, own, above, zeros], axis=1)]
    unnamed x76 -> x38, local copies, waits for them, and re-layouts: 20.4 us -> 8.99 us
    pallas_call x1, Pallas kernels: 92.5 us -> 82.8 us  [adjoint_call(): pl.pallas_call(adjoint_kernel, out_shape=(field, field), in_specs=[SMEM]...]
    pallas_call x1, Pallas kernels: 38.5 us -> 29.4 us  [forward_call(): pl.pallas_call(forward_kernel, out_shape=(jax.ShapeDtypeStruct((rows, cro...]
    ppermute x0 -> x4, local copies, waits for them, and re-layouts: none -> 9 us  [the longest x2 4.56 us: exchange(): from_below = lax.ppermute(top, 'shot', up)]
  transfers between devices with their start and end apart: 7 -> 7, of which waited for: 1 -> 2; matrix products, arithmetic and copies ran while one was open for 13% -> 6% of each run, Pallas kernels for 0% -> 0%
where the time goes in v2:
time: 406 us; the launch traced here: 404 us
  Pallas kernels  112 us (28%)
  blocking collectives  106 us (26%)
  waiting for transfers between devices  93.6 us (23%)
  local copies, waits for them, and re-layouts  33.2 us (8%)
  starting transfers between devices  24.5 us (6%)
  other arithmetic  16.9 us (4%)
  matrix products  14.3 us (4%)
    all_to_all x1, blocking collectives, shards(): lax.all_to_all(returning.reshape(count, capacity, 2 * row_len), 'shot', s...  96 us
    ppermute x3, waiting for transfers between devices, exchange(): from_above = lax.ppermute(bottom, 'shot', down)  93.6 us
    pallas_call x1, Pallas kernels, adjoint_call(): pl.pallas_call(adjoint_kernel, out_shape=(field, field), in_specs=[SMEM]...  82.8 us
    pallas_call x1, Pallas kernels, forward_call(): pl.pallas_call(forward_kernel, out_shape=(jax.ShapeDtypeStruct((rows, cro...  29.4 us
    ppermute x3, starting transfers between devices, exchange(): from_below = lax.ppermute(top, 'shot', up)  10.9 us
    all_to_all x1, blocking collectives, shards(): lax.all_to_all(requests.reshape(count, capacity), 'shot', split_axis=0, c...  10.2 us
    unnamed x38, local copies, waits for them, and re-layouts  8.99 us
  transfers between devices with their start and end apart: 7, of which 2 were waited for; matrix products, arithmetic and copies ran while one was open for 6% of the time, Pallas kernels for 0%

profile of v2, /device:TPU:13, one launch (start us, length us, event | category | flops | bytes accessed | tf_op | source)
XLA Modules:
  0.0 404.2 jit_solution(7576774926571833969)
XLA Ops:
  0.6 0.7 fusion.54
  1.4 0.2 reduce_window_sum.11
  1.5 0.8 select_reduce_fusion
  2.4 0.7 fusion.71
  3.0 1.1 scatter_custom_fusion
  4.2 10.2 %all_to_all.19 = s32[16,1,16]{2,1,0:T(1,128)S(1)} all-to-all(s32[16,1,16]{2,1,0:T(1,128)S(1)} %all_to_all.12), channel_id=1, replica_groups=mesh['groups'=2,'shot'=16] {'shot'}, dimensions={0} | all-to-all | bytes 2048 | tf_op jit(solution)/shard_map/all_to_all | solution.py:361
  14.4 0.5 broadcast.678
  14.9 0.7 reduce.4
  15.7 5.1 %fusion.39 = f32[256,4096]{1,0:T(8,128)} fusion(f32[64,2048]{1,0:T(8,128)} %param.13, f32[64,2048]{1,0:T(8,128)} %param.12, s32[256]{0:T(256)S(1)} %eq.90), kind=kOutput, calls=%fused_computation.58 | convolution fusion | flops 805584896 | bytes 5243904 | tf_op jit(solution)/shard_map/dot_general | solution.py:367
  20.7 7.1 %all-to-all-start.1 = ((f32[16,16,4096]{2,1,0:T(8,128)}), f32[16,16,4096]{2,1,0:T(8,128)}, u32[]{:S(2)}, u32[]{:S(2)}) async-start(f32[16,16,4096]{2,1,0:T(8,128)} %bitcast.111), calls=%async_computation.1 | async-start | bytes 8388608 | tf_op jit(solution)/shard_map/all_to_all | solution.py:368
  28.7 1.0 copy_dynamic-update-slice_fusion.3
  29.8 0.8 copy_dynamic-update-slice_fusion.6
  30.7 0.8 copy_dynamic-update-slice_fusion.5
  31.6 0.8 copy_dynamic-update-slice_fusion.4
  32.4 0.8 copy_dynamic-update-slice_fusion.2
  33.2 0.8 copy_dynamic-update-slice_fusion.1
  33.9 0.8 copy_dynamic-update-slice_fusion
  34.7 0.7 fusion.48
  35.5 2.3 collective-permute-start.1
  37.7 4.2 %collective-permute-start = (f32[128,21,128]{2,0,1:T(8,128)}, f32[128,21,128]{2,0,1:T(8,128)S(1)}, u32[]{:S(2)}, u32[]{:S(2)}) collective-permute-start(f32[128,21,128]{2,0,1:T(8,128)} %get-tuple-element.38), channel_id=1, source_target_pairs={{0,1},{1,2},{2,3},{4,5},{5,6},{6,7},{7,8},{8,9},{9,10},{10,11},{12... | collective-permute-start | bytes 4128776 | tf_op jit(solution)/shard_map/ppermute | solution.py:29
  42.2 0.8 reshape.625.rec_c
  43.1 92.0 %collective-permute-done.1 = f32[128,21,128]{2,0,1:T(8,128)S(1)} collective-permute-done((f32[128,21,128]{2,0,1:T(8,128)}, f32[128,21,128]{2,0,1:T(8,128)S(1)}, u32[]{:S(2)}, u32[]{:S(2)}) %collective-permute-start.1) | collective-permute-done | bytes 1376288 | tf_op jit(solution)/shard_map/ppermute | solution.py:30
  135.1 0.5 slice.207
  136.3 0.5 slice.205
  138.4 3.9 fusion.43
  142.3 0.2 slice_bitcast_fusion
  142.5 0.2 copy.58
  142.7 0.2 copy.59
  143.0 0.6 copy-done
  143.6 0.4 copy-done.2
  144.2 1.0 copy.33
  145.3 2.2 collective-permute-start.2
  147.5 0.2 pad_maximum_fusion.4
  147.6 1.1 copy.34
  148.7 2.3 collective-permute-start.3
  151.1 0.6 reshape.624.src_c
  151.9 0.7 select_n.242.src_v
  152.6 0.2 copy.39
  152.8 0.8 reshape.630.inj_c
  153.6 2.0 copy.35.lo
  155.6 2.0 copy.36.hi
  157.6 2.6 copy.37.m_lo
  160.2 1.6 collective-permute-done.3
  161.8 2.5 copy.38.m_hi
  164.3 29.4 %shard_map.131 = (f32[128,16,128]{2,1,0:T(8,128)}, f32[1024,1,128]{2,1,0:T(1,128)}) custom-call(s32[9]{0:T(128)} %reshape.624.src_c, f32[12]{0:T(128)} %select_n.242.src_v, s32[768]{0:T(1024)} %reshape.625.rec_c, f32[128,16,128]{2,1,0:T(8,128)} %u0.3, f32[128,16,128]{2,1,0:T(8,128)} %um1.3, f32[128,16,128]{2,1,0:T(8,128)} %bitcast.108, ...), custom_call_target="tpu_custom_call" | custom-call | flops 41943040 | bytes 6291456 | tf_op jit(solution)/shard_map/pallas_call | solution.py:272
  193.7 2.9 reduce_sum.22
  196.6 1.9 collective-permute-start.5
  198.6 4.5 %collective-permute-start.4 = (f32[4,256]{1,0:T(4,128)S(1)}, f32[4,256]{1,0:T(4,128)S(1)}, u32[]{:S(2)}, u32[]{:S(2)}) collective-permute-start(f32[4,256]{1,0:T(4,128)S(1)} %bitcast_subtract_fusion), channel_id=1, source_target_pairs={{0,1},{1,2},{2,3},{4,5},{5,6},{6,7},{7,8},{8,9},{9,10},{10,11},{12... | collective-permute-start | bytes 12296 | tf_op jit(solution)/shard_map/ppermute | solution.py:29
  203.1 0.8 slice.220
  204.0 0.8 slice.223
  205.0 3.3 fusion.17
  208.3 0.6 select_n.264.inj_v
  208.9 82.8 %shard_map.132 = (f32[128,32,128]{2,1,0:T(8,128)}, f32[128,32,128]{2,1,0:T(8,128)}) custom-call(s32[9]{0:T(128)} %reshape.624.src_c, f32[12]{0:T(128)} %select_n.242.src_v, s32[2304]{0:T(1024)} %reshape.630.inj_c, f32[3072]{0:T(1024)} %select_n.264.inj_v, f32[128,16,128]{2,1,0:T(8,128)} %u0.3, f32[128,16,128]{2,1,0:T(8,128)} %um1.3, f32[128,16,128]{2,1,0:T(8,128)} %lam5.1, ...), custom_call_target="tpu_custom_call" | custom-call | flops 146800640 | bytes 10485760 | tf_op jit(solution)/shard_map/pallas_call | solution.py:297
  291.7 1.9 fusion.14
  293.5 0.3 copy-done.5
  293.9 0.6 copy-done.6
  294.5 0.3 copy-done.7
  294.8 0.3 copy-done.8
  295.1 4.0 fusion.6
  299.1 1.9 copy.46
  301.0 3.5 fusion.44
  304.5 96.0 %all_to_all.20 = f32[16,16,4096]{2,1,0:T(8,128)S(1)} all-to-all(f32[16,16,4096]{2,1,0:T(8,128)S(1)} %fusion.44), channel_id=1, replica_groups=mesh['groups'=2,'shot'=16] {'shot'}, dimensions={0} | all-to-all | bytes 8388608 | tf_op jit(solution)/shard_map/all_to_all | solution.py:482
  400.5 1.8 convolution_multiply_fusion
  402.3 1.9 reshape.634
  (70 shorter events, 2.2 us)
Async XLA Ops:
  20.7 7.2 %copy-start.11 = (s32[1,256]{1,0:T(1,128)S(1)}, s32[1,256]{1,0:T(1,128)}, u32[]{:S(2)}) copy-start(s32[1,256]{1,0:T(1,128)} %param.22) | copy-start | bytes 3076
  20.7 7.9 %copy-start.3 = (f32[128,16,128]{2,1,0:T(8,128)S(1)}, f32[128,16,128]{2,1,0:T(8,128)}, u32[]{:S(2)}) copy-start(f32[128,16,128]{2,1,0:T(8,128)} %u0.3) | copy-start | bytes 3145732
  20.7 117.6 %all-to-all-start.1 = ((f32[16,16,4096]{2,1,0:T(8,128)}), f32[16,16,4096]{2,1,0:T(8,128)}, u32[]{:S(2)}, u32[]{:S(2)}) async-start(f32[16,16,4096]{2,1,0:T(8,128)} %bitcast.111), calls=%async_computation.1 | async-start | bytes 8388608 | tf_op jit(solution)/shard_map/all_to_all | solution.py:368
  27.9 1.9 copy-start.4
  28.7 1.9 copy-start.9
  29.8 1.7 copy-start.10
  31.5 3.2 copy-start.13
  35.5 99.7 %collective-permute-start.1 = (f32[128,21,128]{2,0,1:T(8,128)}, f32[128,21,128]{2,0,1:T(8,128)S(1)}, u32[]{:S(2)}, u32[]{:S(2)}) collective-permute-start(f32[128,21,128]{2,0,1:T(8,128)} %get-tuple-element.39), channel_id=1, source_target_pairs={{1,0},{2,1},{3,2},{5,4},{6,5},{7,6},{8,7},{9,8},{10,9},{11,10},{13... | collective-permute-start | bytes 4128776 | tf_op jit(solution)/shard_map/ppermute | solution.py:30
  37.7 98.6 %collective-permute-start = (f32[128,21,128]{2,0,1:T(8,128)}, f32[128,21,128]{2,0,1:T(8,128)S(1)}, u32[]{:S(2)}, u32[]{:S(2)}) collective-permute-start(f32[128,21,128]{2,0,1:T(8,128)} %get-tuple-element.38), channel_id=1, source_target_pairs={{0,1},{1,2},{2,3},{4,5},{5,6},{6,7},{7,8},{8,9},{9,10},{10,11},{12... | collective-permute-start | bytes 4128776 | tf_op jit(solution)/shard_map/ppermute | solution.py:29
  142.7 1.0 copy-start
  142.9 1.2 copy-start.2
  145.3 12.3 %collective-permute-start.2 = (f32[128,10,128]{2,0,1:T(8,128)}, f32[128,10,128]{2,0,1:T(8,128)}, u32[]{:S(2)}, u32[]{:S(2)}) collective-permute-start(f32[128,10,128]{2,0,1:T(8,128)} %copy.33), channel_id=1, source_target_pairs={{0,1},{1,2},{2,3},{4,5},{5,6},{6,7},{7,8},{8,9},{9,10},{10,11},{12... | collective-permute-start | bytes 1966088 | tf_op jit(solution)/shard_map/ppermute | solution.py:29
  148.7 13.1 %collective-permute-start.3 = (f32[128,10,128]{2,0,1:T(8,128)}, f32[128,10,128]{2,0,1:T(8,128)}, u32[]{:S(2)}, u32[]{:S(2)}) collective-permute-start(f32[128,10,128]{2,0,1:T(8,128)} %copy.34), channel_id=1, source_target_pairs={{1,0},{2,1},{3,2},{5,4},{6,5},{7,6},{8,7},{9,8},{10,9},{11,10},{13... | collective-permute-start | bytes 1966088 | tf_op jit(solution)/shard_map/ppermute | solution.py:30
  164.3 32.3 %copy-start.12 = (f32[1,4,256]{2,1,0:T(4,128)S(1)}, f32[1,4,256]{2,1,0:T(4,128)}, u32[]{:S(2)}) copy-start(f32[1,4,256]{2,1,0:T(4,128)} %param.23) | copy-start | bytes 12292
  193.7 11.3 %copy-start.1 = (f32[16,8,16,128]{3,2,1,0:T(8,128)S(1)}, f32[16,8,16,128]{3,2,1,0:T(8,128)}, u32[]{:S(2)}) copy-start(f32[16,8,16,128]{3,2,1,0:T(8,128)} %copy-done) | copy-start | bytes 3145732
  196.6 11.6 %collective-permute-start.5 = (f32[4,256]{1,0:T(4,128)S(1)}, f32[4,256]{1,0:T(4,128)S(1)}, u32[]{:S(2)}, u32[]{:S(2)}) collective-permute-start(f32[4,256]{1,0:T(4,128)S(1)} %bitcast_subtract_fusion), channel_id=1, source_target_pairs={{1,0},{2,1},{3,2},{5,4},{6,5},{7,6},{8,7},{9,8},{10,9},{11,10},{13... | collective-permute-start | bytes 12296 | tf_op jit(solution)/shard_map/ppermute | solution.py:30
  198.6 9.7 %collective-permute-start.4 = (f32[4,256]{1,0:T(4,128)S(1)}, f32[4,256]{1,0:T(4,128)S(1)}, u32[]{:S(2)}, u32[]{:S(2)}) collective-permute-start(f32[4,256]{1,0:T(4,128)S(1)} %bitcast_subtract_fusion), channel_id=1, source_target_pairs={{0,1},{1,2},{2,3},{4,5},{5,6},{6,7},{7,8},{8,9},{9,10},{10,11},{12... | collective-permute-start | bytes 12296 | tf_op jit(solution)/shard_map/ppermute | solution.py:29
  291.6 2.2 copy-start.5
  291.7 2.9 copy-start.6
  291.7 3.1 copy-start.7
  291.7 3.4 copy-start.8

commit v3 on v2

--- a/solution.py
+++ b/solution.py
@@ -98,7 +98,7 @@
     lax.fori_loop(0, rows // CX, body, 0)
 
 
-def add_points(buf, slot, coords, vals, base, first, count, checked):
+def add_points(buf, slot, coords, vals, base, first, count):
     depth = buf.shape[-1]
     sub = lax.broadcasted_iota(jnp.int32, (8, depth), 0)
     lane = lax.broadcasted_iota(jnp.int32, (8, depth), 1)
@@ -114,13 +114,10 @@
         buf[slot, x + 1, pl.ds(y8, 8), :] = tile + jnp.where(hit, val, 0.0)
 
     def body(k, carry):
-        if checked:
-            pl.when(coords[3 * k + 1] > 0)(lambda: one(k))
-        else:
-            one(k)
+        one(k)
         return carry
 
-    lax.fori_loop(first, first + count, body, 0, unroll=8)
+    lax.fori_loop(first, first + count, body, 0)
 
 
 def load_padded(buf, slot, own, below, above, k, pad=1):
@@ -165,48 +162,26 @@
     n_src = src_c.shape[0] // 3
     for t in range(steps):
         step_pass(buf, slots[t + 1], slots[t], slots[t + 2], model)
-        add_points(buf, slots[t + 2], src_c, src_v, t * n_src, 0, n_src, False)
+        add_points(buf, slots[t + 2], src_c, src_v, t * n_src, 0, n_src)
         after_step(t, slots[t + 2])
 
 
-def forward_kernel(
-    src_c, src_v, rec_c, u0, um1, sp_own, an_own, lo, hi, m_lo, m_hi, final_out, synth_out, buf, model
-):
+def forward_kernel(src_c, src_v, u0, um1, sp_own, an_own, lo, hi, m_lo, m_hi, waves_out, buf, model):
     zero_edges(buf)
     load_padded(buf, 0, um1, lo, hi, 1)
     load_padded(buf, 1, u0, lo, hi, 0)
     load_model(model, sp_own, an_own, m_lo, m_hi)
-    nrec = rec_c.shape[0] // 3
-    depth = buf.shape[-1]
-    sub = lax.broadcasted_iota(jnp.int32, (8, depth), 0)
-    lane = lax.broadcasted_iota(jnp.int32, (8, depth), 1)
+    rows, cross = u0.shape[0], u0.shape[1]
 
     def after_step(t, slot):
-        def body(r, carry):
-            x = rec_c[3 * r]
-            y = rec_c[3 * r + 1]
-            z = rec_c[3 * r + 2]
-            y8 = pl.multiple_of((y // 8) * 8, 8)
-            tile = buf[slot, x + 1, pl.ds(y8, 8), :]
-            hit = (sub == y - y8) & (lane == z)
-            synth_out[t * nrec + r] = jnp.sum(jnp.where(hit, tile, 0.0), axis=0, keepdims=True)
+        def body(i, carry):
+            x0 = pl.multiple_of(i * CX, CX)
+            waves_out[t, pl.ds(x0, CX)] = buf[slot, pl.ds(x0 + 1, CX), MARGIN : MARGIN + cross]
             return carry
 
-        lax.fori_loop(0, nrec, body, 0, unroll=8)
-
-    slots = [0, 1, 2, 0, 1, 2]
-    run_forward(buf, slots, src_c, src_v, model, after_step, STEPS)
-    rows = u0.shape[0]
-    cross = final_out.shape[1]
-    lo = (buf.shape[2] - cross) // 2
-    last = slots[STEPS + 1]
-
-    def body(i, carry):
-        x0 = pl.multiple_of(i * CX, CX)
-        final_out[pl.ds(x0, CX)] = buf[last, pl.ds(x0 + 1, CX), lo : lo + cross]
-        return carry
-
-    lax.fori_loop(0, rows // CX, body, 0)
+        lax.fori_loop(0, rows // CX, body, 0)
+
+    run_forward(buf, [0, 1, 2, 0, 1, 2], src_c, src_v, model, after_step, STEPS)
 
 
 def adjoint_kernel(
@@ -222,15 +197,14 @@
     load_padded(lams, 0, lam6, lo, hi, 3)
     load_padded(lams, 1, lam5, lo, hi, 2)
     rows = u0.shape[0]
-    n_inj = inj_c.shape[0] // 3
-    n_own = n_inj // 3
+    n_inj = inj_c.shape[0] // 3 - 1
+    n_valid = inj_c[3 * n_inj]
     order = [0, 1, 2, 0, 1, 2]
     for k in range(STEPS):
         t = STEPS - 1 - k
         later, now, new = order[k], order[k + 1], order[k + 2]
         step_pass(lams, now, later, new, model)
-        add_points(lams, new, inj_c, inj_v, t * n_inj, 0, n_own, False)
-        add_points(lams, new, inj_c, inj_v, t * n_inj, n_own, n_inj - n_own, True)
+        add_points(lams, new, inj_c, inj_v, t * n_inj, 0, n_valid)
         wave = t + 1
 
         def body(i, carry, new=new, wave=wave, first=(k == 0)):
@@ -265,18 +239,14 @@
 PARAMS = pltpu.CompilerParams(vmem_limit_bytes=62 * 1024 * 1024)
 
 
-def forward_call(src_c, src_v, rec_c, u0, um1, sp_own, an_own, lo, hi, m_lo, m_hi):
+def forward_call(src_c, src_v, u0, um1, sp_own, an_own, lo, hi, m_lo, m_hi):
     rows, cross, depth = u0.shape
     wide = cross + 2 * MARGIN
-    nrec = rec_c.shape[0] // 3
     return pl.pallas_call(
         forward_kernel,
-        out_shape=(
-            jax.ShapeDtypeStruct((rows, cross, depth), jnp.float32),
-            jax.ShapeDtypeStruct((STEPS * nrec, 1, depth), jnp.float32),
-        ),
-        in_specs=[SMEM] * 3 + [VMEM] * 8,
-        out_specs=(VMEM, VMEM),
+        out_shape=jax.ShapeDtypeStruct((STEPS, rows, cross, depth), jnp.float32),
+        in_specs=[SMEM] * 2 + [VMEM] * 8,
+        out_specs=VMEM,
         scratch_shapes=[
             pltpu.VMEM((3, rows + 2, wide, depth), jnp.float32),
             pltpu.VMEM((2, rows, wide, depth), jnp.float32),
@@ -284,10 +254,10 @@
         compiler_params=PARAMS,
         cost_estimate=pl.CostEstimate(
             flops=STEPS * 20 * rows * wide * depth,
-            bytes_accessed=6 * rows * cross * depth * 4,
+            bytes_accessed=8 * rows * cross * depth * 4,
             transcendentals=0,
         ),
-    )(src_c, src_v, rec_c, u0, um1, sp_own, an_own, lo, hi, m_lo, m_hi)
+    )(src_c, src_v, u0, um1, sp_own, an_own, lo, hi, m_lo, m_hi)
 
 
 def adjoint_call(src_c, src_v, inj_c, inj_v, u0, um1, lam5, lam6, sp_own, an_own, lo, hi, m_lo, m_hi):
@@ -420,19 +390,25 @@
     valid_src = (sy >= 0) & (sy < wide_y)
     src_coords = jnp.stack([sx, jnp.where(valid_src, sy, 0), sz], axis=1).reshape(-1)
     src_vals = jnp.where(valid_src[None, :], wav_all, 0.0).reshape(-1)
-    rec_coords = jnp.stack([rx_own, ry_own, rz_own], axis=1).reshape(-1)
     halos = (from_below, from_above, model_below, model_above)
-    final_wide, synth_rows = forward_call(
-        src_coords, src_vals, rec_coords, state_now, state_prev, speed_own, aniso_own, *halos
-    )
-    final_wave = final_wide
-    synthetic = jnp.sum(synth_rows, axis=-1).reshape(STEPS, nrec)
+    waves_own = forward_call(src_coords, src_vals, state_now, state_prev, speed_own, aniso_own, *halos)
+    final_wave = waves_own[STEPS - 1]
+    flat_cells = (
+        jnp.arange(STEPS, dtype=jnp.int32)[:, None] * (rows * row_len) + receiver_cell[0][None, :]
+    )
+    synthetic = waves_own.reshape(-1)[flat_cells]
     misfit_own = synthetic - observed[0]
     mis_below, mis_above = exchange(misfit_own, misfit_own, count)
     valid_rec = (ry >= MARGIN - HALO + 1) & (ry < MARGIN + cross + HALO - 1)
-    inj_coords = jnp.stack([rx, jnp.where(valid_rec, ry, 0), rz], axis=1).reshape(-1)
+    valid_rec = valid_rec.at[:nrec].set(True)
+    total = 3 * nrec
+    dest = jnp.where(valid_rec, jnp.cumsum(valid_rec.astype(jnp.int32)) - 1, total)
+    coords = jnp.stack([rx, ry, rz], axis=1)
+    inj_coords = jnp.zeros((total + 1, 3), jnp.int32).at[dest].set(coords, mode="drop")
+    inj_coords = inj_coords.at[total, 0].set(jnp.sum(valid_rec.astype(jnp.int32)))
+    inj_coords = inj_coords.reshape(-1)
     injected = jnp.concatenate([misfit_own, mis_below, mis_above], axis=1)
-    inj_vals = jnp.where(valid_rec[None, :], injected, 0.0).reshape(-1)
+    inj_vals = jnp.zeros((STEPS, total), jnp.float32).at[:, dest].set(injected, mode="drop").reshape(-1)
     gradient_speed, gradient_aniso = adjoint_call(
         src_coords, src_vals, inj_coords, inj_vals, state_now, state_prev, adjoint_now, adjoint_prev,
         speed_own, aniso_own, *halos

time: 406 us -> 415 us (1.022)
  blocking collectives: 106 us -> 10.2 us
  waiting for transfers between devices: 93.6 us -> 183 us
  local copies, waits for them, and re-layouts: 33.2 us -> 57.9 us
  Pallas kernels: 112 us -> 92.7 us
  starting transfers between devices: 24.5 us -> 33.4 us
    all_to_all x1 -> x0, blocking collectives: 96 us -> none  [shards(): lax.all_to_all(returning.reshape(count, capacity, 2 * row_len), 'shot', s...]
    all_to_all x0 -> x1, waiting for transfers between devices: none -> 90.2 us  [shards(): lax.all_to_all(returning.reshape(count, capacity, 2 * row_len), 'shot', s...]
    gather x0 -> x2, local copies, waits for them, and re-layouts: none -> 12.5 us  [shards(): synthetic = waves_own.reshape(-1)[flat_cells]]
    pallas_call x1, Pallas kernels: 82.8 us -> 70.6 us  [adjoint_call(): pl.pallas_call(adjoint_kernel, out_shape=(field, field), in_specs=[SMEM]...]
    scatter x0 -> x5, local copies, waits for them, and re-layouts: none -> 10 us  [the longest x2 4.53 us: shards(): jnp.zeros((STEPS, total), jnp.float32).at[:, dest]]
    all_to_all x0 -> x1, starting transfers between devices: none -> 9.04 us  [shards(): lax.all_to_all(returning.reshape(count, capacity, 2 * row_len), 'shot', s...]
    pallas_call x1, Pallas kernels: 29.4 us -> 22.1 us  [forward_call(): pl.pallas_call(forward_kernel, out_shape=jax.ShapeDtypeStruct((STEPS, row...]
    unnamed x38 -> x53, local copies, waits for them, and re-layouts: 8.99 us -> 8.96 us
  transfers between devices with their start and end apart: 7 -> 8, of which waited for: 2 -> 2; matrix products, arithmetic and copies ran while one was open for 6% -> 8% of each run, Pallas kernels for 0% -> 0%
where the time goes in v3:
time: 415 us; the launch traced here: 414 us
  waiting for transfers between devices  183 us (44%)
  Pallas kernels  92.7 us (22%)
  local copies, waits for them, and re-layouts  57.9 us (14%)
  starting transfers between devices  33.4 us (8%)
  matrix products  18.3 us (4%)
  other arithmetic  15.6 us (4%)
  blocking collectives  10.2 us (2%)
    ppermute x3, waiting for transfers between devices, exchange(): from_above = lax.ppermute(bottom, 'shot', down)  92.4 us
    all_to_all x1, waiting for transfers between devices, shards(): lax.all_to_all(returning.reshape(count, capacity, 2 * row_len), 'shot', s...  90.2 us
    pallas_call x1, Pallas kernels, adjoint_call(): pl.pallas_call(adjoint_kernel, out_shape=(field, field), in_specs=[SMEM]...  70.6 us
    pallas_call x1, Pallas kernels, forward_call(): pl.pallas_call(forward_kernel, out_shape=jax.ShapeDtypeStruct((STEPS, row...  22.1 us
    gather x2, local copies, waits for them, and re-layouts, shards(): synthetic = waves_own.reshape(-1)[flat_cells]  12.5 us
    ppermute x3, starting transfers between devices, exchange(): from_below = lax.ppermute(top, 'shot', up)  10.9 us
    all_to_all x1, blocking collectives, shards(): lax.all_to_all(requests.reshape(count, capacity), 'shot', split_axis=0, c...  10.2 us
    all_to_all x1, starting transfers between devices, shards(): lax.all_to_all(returning.reshape(count, capacity, 2 * row_len), 'shot', s...  9.04 us
  transfers between devices with their start and end apart: 8, of which 2 were waited for; matrix products, arithmetic and copies ran while one was open for 8% of the time, Pallas kernels for 0%

profile of v3, /device:TPU:13, one launch (start us, length us, event | category | flops | bytes accessed | tf_op | source)
XLA Modules:
  0.0 414.0 jit_solution(1064517898826813027)
XLA Ops:
  0.6 0.7 fusion.58
  1.5 0.8 select_reduce_fusion
  2.4 0.7 fusion.72
  3.0 1.1 scatter_custom_fusion
  4.3 10.2 %all_to_all.19 = s32[16,1,16]{2,1,0:T(1,128)S(1)} all-to-all(s32[16,1,16]{2,1,0:T(1,128)S(1)} %all_to_all.12), channel_id=1, replica_groups=mesh['groups'=2,'shot'=16] {'shot'}, dimensions={0} | all-to-all | bytes 2048 | tf_op jit(solution)/shard_map/all_to_all | solution.py:331
  14.4 0.5 broadcast.420
  14.9 0.7 reduce.9
  15.7 5.0 %fusion.39 = f32[256,4096]{1,0:T(8,128)} fusion(f32[64,2048]{1,0:T(8,128)} %param.17, f32[64,2048]{1,0:T(8,128)} %param.16, s32[256]{0:T(256)S(1)} %eq.90), kind=kOutput, calls=%fused_computation.62 | convolution fusion | flops 805584896 | bytes 5243904 | tf_op jit(solution)/shard_map/dot_general | solution.py:337
  20.7 7.1 %all-to-all-start.1 = ((f32[16,16,4096]{2,1,0:T(8,128)}), f32[16,16,4096]{2,1,0:T(8,128)}, u32[]{:S(2)}, u32[]{:S(2)}) async-start(f32[16,16,4096]{2,1,0:T(8,128)} %bitcast.103), calls=%async_computation.1 | async-start | bytes 8388608 | tf_op jit(solution)/shard_map/all_to_all | solution.py:338
  28.7 1.0 copy_dynamic-update-slice_fusion.3
  29.8 0.8 copy_dynamic-update-slice_fusion.6
  30.7 0.8 copy_dynamic-update-slice_fusion.5
  31.6 0.8 copy_dynamic-update-slice_fusion.4
  32.4 0.8 copy_dynamic-update-slice_fusion.2
  33.2 0.8 copy_dynamic-update-slice_fusion.1
  34.0 0.8 copy_dynamic-update-slice_fusion
  34.8 0.7 fusion.52
  35.5 2.3 collective-permute-start.1
  37.8 4.2 %collective-permute-start = (f32[128,21,128]{2,0,1:T(8,128)}, f32[128,21,128]{2,0,1:T(8,128)S(1)}, u32[]{:S(2)}, u32[]{:S(2)}) collective-permute-start(f32[128,21,128]{2,0,1:T(8,128)} %get-tuple-element.58), channel_id=1, source_target_pairs={{0,1},{1,2},{2,3},{4,5},{5,6},{6,7},{7,8},{8,9},{9,10},{10,11},{12... | collective-permute-start | bytes 4128776 | tf_op jit(solution)/shard_map/ppermute | solution.py:29
  42.1 0.6 slice_bitcast_fusion.8
  42.8 92.4 %collective-permute-done.1 = f32[128,21,128]{2,0,1:T(8,128)S(1)} collective-permute-done((f32[128,21,128]{2,0,1:T(8,128)}, f32[128,21,128]{2,0,1:T(8,128)S(1)}, u32[]{:S(2)}, u32[]{:S(2)}) %collective-permute-start.1) | collective-permute-done | bytes 1376288 | tf_op jit(solution)/shard_map/ppermute | solution.py:30
  135.1 0.5 slice.253
  136.3 0.5 slice.251
  138.0 0.7 reshape.412.src_c
  139.0 0.6 select_n.177.src_v
  140.1 0.3 reduce-window.9
  140.5 3.9 fusion.47
  145.2 0.6 copy-done
  145.8 0.3 copy-done.2
  146.3 1.0 copy.40
  147.3 2.2 collective-permute-start.2
  149.7 1.0 copy.41
  150.7 2.1 collective-permute-start.3
  153.2 1.3 compare_select_fusion
  154.5 4.4 %scatter_custom_fusion.1 = s32[769,3]{1,0:T(8,128)S(1)} fusion(s32[768]{0:T(1024)} %get-tuple-element.57, s32[768,3]{1,0:T(8,128)S(1)} %copy.46, s32[]{:T(128)} %constant.273.clone.1), kind=kCustom, calls=%fused_computation.76 | custom fusion | bytes 9740 | tf_op jit(solution)/shard_map/scatter | solution.py:407
  158.9 0.9 scatter.34
  159.8 0.8 reshape.420.inj_c
  160.6 2.0 copy.42.lo
  162.7 2.0 copy.43.hi
  164.6 2.5 copy.44.m_lo
  167.1 2.5 copy.45.m_hi
  169.6 22.1 %shard_map.131 = f32[4,128,16,128]{3,2,1,0:T(8,128)} custom-call(s32[9]{0:T(128)} %reshape.412.src_c, f32[12]{0:T(128)} %select_n.177.src_v, f32[128,16,128]{2,1,0:T(8,128)} %u0.3, f32[128,16,128]{2,1,0:T(8,128)} %um1.3, f32[128,16,128]{2,1,0:T(8,128)} %bitcast.99, f32[128,16,128]{2,1,0:T(8,128)} %bitcast.105, f32[128,21,128]{2,1,0:T(8,128)} %copy.42.lo, ...), custom_call_target="tpu_custom_call" | custom-call | flops 41943040 | bytes 8388608 | tf_op jit(solution)/shard_map/pallas_call | solution.py:245
  191.8 12.5 %gather_fusion = f32[1024]{0:T(1024)S(1)} fusion(f32[1048576]{0:T(1024)} %bitcast.102, s32[1024]{0:T(1024)S(1)} %broadcast_clamp_fusion), kind=kCustom, calls=%fused_computation | custom fusion | bytes 12288 | tf_op jit(solution)/shard_map/gather | solution.py:399
  204.3 1.9 collective-permute-start.5
  206.2 4.5 %collective-permute-start.4 = (f32[4,256]{1,0:T(4,128)S(1)}, f32[4,256]{1,0:T(4,128)S(1)}, u32[]{:S(2)}, u32[]{:S(2)}) collective-permute-start(f32[4,256]{1,0:T(4,128)S(1)} %bitcast_subtract_fusion), channel_id=1, source_target_pairs={{0,1},{1,2},{2,3},{4,5},{5,6},{6,7},{7,8},{8,9},{9,10},{10,11},{12... | collective-permute-start | bytes 12296 | tf_op jit(solution)/shard_map/ppermute | solution.py:29
  210.8 0.8 slice.267
  211.6 0.8 slice.270
  212.6 3.3 fusion.17
  216.1 4.4 %scatter_custom_fusion.2 = f32[4,768]{0,1:T(8,128)S(1)} fusion(s32[768]{0:T(1024)} %get-tuple-element.56, f32[768,4]{1,0:T(8,128)S(1)} %copy.47, f32[]{:T(128)} %constant.277.clone.1), kind=kCustom, calls=%fused_computation.78 | custom fusion | bytes 12800 | tf_op jit(solution)/shard_map/scatter | solution.py:411
  220.7 0.6 reshape.422.inj_v
  221.3 70.6 %shard_map.132 = (f32[128,32,128]{2,1,0:T(8,128)}, f32[128,32,128]{2,1,0:T(8,128)}) custom-call(s32[9]{0:T(128)} %reshape.412.src_c, f32[12]{0:T(128)} %select_n.177.src_v, s32[2307]{0:T(1024)} %reshape.420.inj_c, f32[3072]{0:T(1024)} %reshape.422.inj_v, f32[128,16,128]{2,1,0:T(8,128)} %u0.3, f32[128,16,128]{2,1,0:T(8,128)} %um1.3, f32[128,16,128]{2,1,0:T(8,128)} %lam5.1, ...), custom_call_target="tpu_custom_call" | custom-call | flops 146800640 | bytes 10485760 | tf_op jit(solution)/shard_map/pallas_call | solution.py:267
  291.9 1.9 fusion.14
  293.8 0.3 copy-done.5
  294.1 0.6 copy-done.6
  294.8 0.3 copy-done.7
  295.0 0.3 copy-done.8
  295.3 4.0 fusion.6
  299.3 1.9 copy.55
  301.3 5.4 %fusion.48 = f32[16,16,4096]{2,1,0:T(8,128)} fusion(f32[128,4096,1]{0,1,2:T(8,128)} %bitcast.111, s32[16,16]{1,0:T(8,128)S(1)} %multiply_add_fusion, s32[128]{0:T(128)S(1)} %copy-done.15), kind=kOutput, calls=%fused_computation.83 | convolution fusion | flops 1610645504 | bytes 6292992 | tf_op jit(solution)/shard_map/dot_general | solution.py:457
  306.7 9.0 %all-to-all-start.2 = ((f32[16,16,4096]{2,1,0:T(8,128)}), f32[16,16,4096]{2,1,0:T(8,128)}, u32[]{:S(2)}, u32[]{:S(2)}) async-start(f32[16,16,4096]{2,1,0:T(8,128)} %fusion.48), calls=%async_computation.2 | async-start | bytes 8388608 | tf_op jit(solution)/shard_map/all_to_all | solution.py:458
  315.7 2.3 slice_bitcast_fusion
  318.0 90.2 %all-to-all-done.2 = f32[16,16,4096]{2,1,0:T(8,128)} async-done(((f32[16,16,4096]{2,1,0:T(8,128)}), f32[16,16,4096]{2,1,0:T(8,128)}, u32[]{:S(2)}, u32[]{:S(2)}) %all-to-all-start.2) | async-done | bytes 4194336 | tf_op jit(solution)/shard_map/all_to_all | solution.py:458
  408.2 4.0 convolution_multiply_fusion
  412.1 1.9 reshape.425
  (98 shorter events, 4.0 us)
Async XLA Ops:
  3.0 137.4 %copy-start.14 = (s32[128]{0:T(128)}, s32[128]{0:T(128)S(1)}, u32[]{:S(2)}) copy-start(s32[128]{0:T(128)S(1)} %get-tuple-element.64) | copy-start | bytes 1540
  15.7 5.0 %copy-start.12 = (s32[256]{0:T(256)}, s32[256]{0:T(256)S(1)}, u32[]{:S(2)}) copy-start(s32[256]{0:T(256)S(1)} %eq.90) | copy-start | bytes 3076
  20.7 7.2 %copy-start.11 = (s32[1,256]{1,0:T(1,128)S(1)}, s32[1,256]{1,0:T(1,128)}, u32[]{:S(2)}) copy-start(s32[1,256]{1,0:T(1,128)} %param.26) | copy-start | bytes 3076
  20.7 7.9 %copy-start.3 = (f32[128,16,128]{2,1,0:T(8,128)S(1)}, f32[128,16,128]{2,1,0:T(8,128)}, u32[]{:S(2)}) copy-start(f32[128,16,128]{2,1,0:T(8,128)} %u0.3) | copy-start | bytes 3145732
  20.7 119.8 %all-to-all-start.1 = ((f32[16,16,4096]{2,1,0:T(8,128)}), f32[16,16,4096]{2,1,0:T(8,128)}, u32[]{:S(2)}, u32[]{:S(2)}) async-start(f32[16,16,4096]{2,1,0:T(8,128)} %bitcast.103), calls=%async_computation.1 | async-start | bytes 8388608 | tf_op jit(solution)/shard_map/all_to_all | solution.py:338
  27.9 1.8 copy-start.4
  28.7 1.9 copy-start.9
  29.8 1.7 copy-start.10
  31.6 3.2 copy-start.20
  35.5 99.6 %collective-permute-start.1 = (f32[128,21,128]{2,0,1:T(8,128)}, f32[128,21,128]{2,0,1:T(8,128)S(1)}, u32[]{:S(2)}, u32[]{:S(2)}) collective-permute-start(f32[128,21,128]{2,0,1:T(8,128)} %get-tuple-element.59), channel_id=1, source_target_pairs={{1,0},{2,1},{3,2},{5,4},{6,5},{7,6},{8,7},{9,8},{10,9},{11,10},{13... | collective-permute-start | bytes 4128776 | tf_op jit(solution)/shard_map/ppermute | solution.py:30
  37.8 98.6 %collective-permute-start = (f32[128,21,128]{2,0,1:T(8,128)}, f32[128,21,128]{2,0,1:T(8,128)S(1)}, u32[]{:S(2)}, u32[]{:S(2)}) collective-permute-start(f32[128,21,128]{2,0,1:T(8,128)} %get-tuple-element.58), channel_id=1, source_target_pairs={{0,1},{1,2},{2,3},{4,5},{5,6},{6,7},{7,8},{8,9},{9,10},{10,11},{12... | collective-permute-start | bytes 4128776 | tf_op jit(solution)/shard_map/ppermute | solution.py:29
  144.8 1.0 copy-start
  145.0 1.1 copy-start.2
  147.3 17.3 %collective-permute-start.2 = (f32[128,10,128]{2,0,1:T(8,128)}, f32[128,10,128]{2,0,1:T(8,128)}, u32[]{:S(2)}, u32[]{:S(2)}) collective-permute-start(f32[128,10,128]{2,0,1:T(8,128)} %copy.40), channel_id=1, source_target_pairs={{0,1},{1,2},{2,3},{4,5},{5,6},{6,7},{7,8},{8,9},{9,10},{10,11},{12... | collective-permute-start | bytes 1966088 | tf_op jit(solution)/shard_map/ppermute | solution.py:29
  150.7 16.4 %collective-permute-start.3 = (f32[128,10,128]{2,0,1:T(8,128)}, f32[128,10,128]{2,0,1:T(8,128)}, u32[]{:S(2)}, u32[]{:S(2)}) collective-permute-start(f32[128,10,128]{2,0,1:T(8,128)} %copy.41), channel_id=1, source_target_pairs={{1,0},{2,1},{3,2},{5,4},{6,5},{7,6},{8,7},{9,8},{10,9},{11,10},{13... | collective-permute-start | bytes 1966088 | tf_op jit(solution)/shard_map/ppermute | solution.py:30
  191.7 12.6 %copy-start.16 = (f32[1,4,256]{2,1,0:T(4,128)S(1)}, f32[1,4,256]{2,1,0:T(4,128)}, u32[]{:S(2)}) copy-start(f32[1,4,256]{2,1,0:T(4,128)} %param.27) | copy-start | bytes 12292
  191.7 20.7 %copy-start.19 = (f32[16]{0:T(128)S(1)}, f32[16]{0:T(128)}, u32[]{:S(2)}) copy-start(f32[16]{0:T(128)} %get-tuple-element.68) | copy-start | bytes 196
  191.7 20.9 %copy-start.1 = (f32[16,8,16,128]{3,2,1,0:T(8,128)S(1)}, f32[16,8,16,128]{3,2,1,0:T(8,128)}, u32[]{:S(2)}) copy-start(f32[16,8,16,128]{3,2,1,0:T(8,128)} %copy-done) | copy-start | bytes 3145732
  191.7 20.9 %copy-start.17 = (f32[16]{0:T(128)S(1)}, f32[16]{0:T(128)}, u32[]{:S(2)}) copy-start(f32[16]{0:T(128)} %get-tuple-element.66) | copy-start | bytes 196
  191.7 20.9 %copy-start.18 = (f32[16]{0:T(128)S(1)}, f32[16]{0:T(128)}, u32[]{:S(2)}) copy-start(f32[16]{0:T(128)} %get-tuple-element.67) | copy-start | bytes 196
  204.3 11.6 %collective-permute-start.5 = (f32[4,256]{1,0:T(4,128)S(1)}, f32[4,256]{1,0:T(4,128)S(1)}, u32[]{:S(2)}, u32[]{:S(2)}) collective-permute-start(f32[4,256]{1,0:T(4,128)S(1)} %bitcast_subtract_fusion), channel_id=1, source_target_pairs={{1,0},{2,1},{3,2},{5,4},{6,5},{7,6},{8,7},{9,8},{10,9},{11,10},{13... | collective-permute-start | bytes 12296 | tf_op jit(solution)/shard_map/ppermute | solution.py:30
  206.2 9.7 %collective-permute-start.4 = (f32[4,256]{1,0:T(4,128)S(1)}, f32[4,256]{1,0:T(4,128)S(1)}, u32[]{:S(2)}, u32[]{:S(2)}) collective-permute-start(f32[4,256]{1,0:T(4,128)S(1)} %bitcast_subtract_fusion), channel_id=1, source_target_pairs={{0,1},{1,2},{2,3},{4,5},{5,6},{6,7},{7,8},{8,9},{9,10},{10,11},{12... | collective-permute-start | bytes 12296 | tf_op jit(solution)/shard_map/ppermute | solution.py:29
  291.9 2.2 copy-start.5
  291.9 2.9 copy-start.6
  291.9 3.1 copy-start.7
  291.9 3.4 copy-start.8
  299.3 1.9 copy-start.15
  306.7 101.5 %all-to-all-start.2 = ((f32[16,16,4096]{2,1,0:T(8,128)}), f32[16,16,4096]{2,1,0:T(8,128)}, u32[]{:S(2)}, u32[]{:S(2)}) async-start(f32[16,16,4096]{2,1,0:T(8,128)} %fusion.48), calls=%async_computation.2 | async-start | bytes 8388608 | tf_op jit(solution)/shard_map/all_to_all | solution.py:458
  315.7 92.5 %copy-start.13 = (s32[256]{0:T(256)S(1)}, s32[256]{0:T(256)}, u32[]{:S(2)}) copy-start(s32[256]{0:T(256)} %copy-done.12) | copy-start | bytes 3076
